TPU v7x, 256 devices: a whole 4x4x8 slice. The times are simulated.
256 devices in a mesh: lat: 16 (over y, x_lo, core), lon: 16 (over x_hi, z).
Axes of the slice: x: 4 (x_hi: 2, x_lo: 2; x = x_hi * 2 + x_lo), y: 4, z: 8, core: 2. Of those that a mesh axis runs over, the one named last changes fastest.
Arguments:
- fields: bfloat16 [64, 2048, 192], P('lat', 'lon'), may hold values from -6 to 6
- kernel_first: bfloat16 [9, 192, 192], replicated, may hold values from -0.15625 to 0.15625
- kernel_second: bfloat16 [9, 192, 192], replicated, may hold values from -0.15625 to 0.15625
- kernel_third: bfloat16 [9, 192, 192], replicated, may hold values from -0.15625 to 0.15625
- cotangent: bfloat16 [64, 2048, 192], P('lat', 'lon'), may hold values from -6 to 6
Outputs:
- output: float32 [64, 2048, 192], P('lat', 'lon')
- field_grad: float32 [64, 2048, 192], P('lat', 'lon')
- grad_first: float32 [9, 192, 192], P(None, None, 'lat')
- grad_second: float32 [9, 192, 192], P(None, None, 'lat')
- grad_third: float32 [9, 192, 192], P(None, None, 'lat')
All inputs are finite; a program needn't handle non-finite values.
Results may differ from a plain program's by a relative error of at most 0.0049.
Values may be sent and summed in bfloat16 or wider, within the bound.
No kernel may reach another device: no remote copies, remote signals or barrier semaphores. Data moves between devices by JAX's collectives and lax.ppermute only.
A program may use at most 64 MiB of HBM per device.

v0:
```python
import jax
import jax.numpy as jnp
from jax import lax
from jax.sharding import PartitionSpec as P


def exchange(x, h):
    nlat, nlon = lax.axis_size("lat"), lax.axis_size("lon")
    left = lax.ppermute(x[:, -h:], "lon", [(j, (j + 1) % nlon) for j in range(nlon)])
    right = lax.ppermute(x[:, :h], "lon", [(j, (j - 1) % nlon) for j in range(nlon)])
    x = jnp.concatenate([left, x, right], axis=1)
    top = lax.ppermute(x[-h:], "lat", [(i, i + 1) for i in range(nlat - 1)])
    bottom = lax.ppermute(x[:h], "lat", [(i + 1, i) for i in range(nlat - 1)])
    return jnp.concatenate([top, x, bottom], axis=0)


def inside(x, own_rows, h):
    first = lax.axis_index("lat") * own_rows - h
    rows = first + lax.broadcasted_iota(jnp.int32, (x.shape[0], 1, 1), 0)
    keep = (rows >= 0) & (rows < own_rows * lax.axis_size("lat"))
    return jnp.where(keep, x, jnp.zeros_like(x))


def crop(x, h):
    return x[h : x.shape[0] - h, h : x.shape[1] - h]


def gelu(z):
    return 0.5 * z * (1.0 + jax.scipy.special.erf(z * 0.7071067811865476))


def gelu_slope(z):
    return (
        0.5 * (1.0 + jax.scipy.special.erf(z * 0.7071067811865476))
        + z * jnp.exp(-0.5 * z * z) * 0.3989422804014327
    )


def forward_conv(padded, kernel):
    taps, n_in, n_out = kernel.shape
    w = kernel.reshape(3, 3, n_in, n_out)
    return lax.conv_general_dilated(
        padded[None], w, (1, 1), "VALID", dimension_numbers=("NHWC", "HWIO", "NHWC"),
        preferred_element_type=jnp.float32,
    )[0]


def adjoint_conv(padded, kernel):
    taps, n_in, n_out = kernel.shape
    w = kernel.reshape(3, 3, n_in, n_out)[::-1, ::-1].transpose(0, 1, 3, 2)
    return lax.conv_general_dilated(
        padded[None], w, (1, 1), "VALID", dimension_numbers=("NHWC", "HWIO", "NHWC"),
        preferred_element_type=jnp.float32,
    )[0]


def halve(x, axis):
    n = lax.axis_size(axis)
    bits = n.bit_length() - 1
    me = lax.axis_index(axis)
    x = x.reshape((2,) * bits + x.shape[1:])
    x = x.transpose(tuple(range(bits - 1, -1, -1)) + tuple(range(bits, x.ndim)))
    for b in range(bits):
        mine = (me >> b) & 1
        keep = lax.dynamic_index_in_dim(x, mine, 0, keepdims=False)
        send = lax.dynamic_index_in_dim(x, 1 - mine, 0, keepdims=False)
        x = keep + lax.ppermute(send, axis, [(i, i ^ (1 << b)) for i in range(n)])
    return x


def all_sum(x, axis):
    n = lax.axis_size(axis)
    for b in range(n.bit_length() - 1):
        x = x + lax.ppermute(x, axis, [(i, i ^ (1 << b)) for i in range(n)])
    return x


def kernel_grad(padded, delta):
    own_rows, own_cols = (delta.shape[0], delta.shape[1])
    cells = own_rows * lax.axis_size("lat") * own_cols * lax.axis_size("lon")
    scale = 1.0 / float(cells) ** 0.5
    terms = []
    for tap in range(9):
        shift_a, shift_b = divmod(tap, 3)
        piece = padded[shift_a : shift_a + own_rows, shift_b : shift_b + own_cols]
        terms.append(
            jnp.einsum("rci,rco->oi", piece, delta, preferred_element_type=jnp.float32) * scale
        )
    local_term = jnp.stack(terms, axis=1)
    n_out, taps, n_in = local_term.shape
    nlat = lax.axis_size("lat")
    owned = halve(local_term.reshape(nlat, (n_out // nlat) * taps * n_in), "lat")
    owned = all_sum(owned, "lon")
    return owned.reshape(n_out // nlat, taps, n_in).transpose(1, 2, 0)


def on_device(fields, kernel_first, kernel_second, kernel_third, cotangent):
    own_rows = fields.shape[0]
    width = fields.shape[2]
    both = exchange(jnp.concatenate([fields, cotangent], axis=2), 4)
    fields_4, cotangent_3 = both[..., :width], crop(both[..., width:], 1)
    pre_first = forward_conv(fields_4, kernel_first)
    act_first = inside(gelu(pre_first).astype(jnp.bfloat16), own_rows, 3)
    pre_second = forward_conv(act_first, kernel_second)
    act_second = inside(gelu(crop(pre_second, 1)).astype(jnp.bfloat16), own_rows, 1)
    output = forward_conv(act_second, kernel_third)
    grad_third = kernel_grad(act_second, crop(cotangent_3, 3))
    delta_second = inside(
        (adjoint_conv(cotangent_3, kernel_third) * gelu_slope(pre_second)).astype(jnp.bfloat16),
        own_rows, 2,
    )
    delta_first = inside(
        (adjoint_conv(delta_second, kernel_second) * gelu_slope(crop(pre_first, 2))).astype(
            jnp.bfloat16
        ),
        own_rows, 1,
    )
    grad_second = kernel_grad(crop(act_first, 2), crop(delta_second, 2))
    field_grad = adjoint_conv(delta_first, kernel_first)
    grad_first = kernel_grad(crop(fields_4, 3), crop(delta_first, 1))
    return (output, field_grad, grad_first, grad_second, grad_third)


def solution(mesh):
    in_specs = (P("lat", "lon", None), P(), P(), P(), P("lat", "lon", None))
    out_specs = (
        P("lat", "lon", None),
        P("lat", "lon", None),
        P(None, None, "lat"),
        P(None, None, "lat"),
        P(None, None, "lat"),
    )
    return jax.shard_map(
        on_device, mesh=mesh, in_specs=in_specs, out_specs=out_specs, check_vma=False
    )
```

profile of v0, /device:TPU:24, one launch (start us, length us, event | category | flops | bytes accessed | tf_op | source)
XLA Modules:
  0.0 221.5 jit_solution(1722734726567187663)
XLA Ops:
  4.8 6.5 %collective-permute-start.1 = (bf16[4,4,384]{1,2,0:T(8,128)(2,1)S(1)}, bf16[4,4,384]{1,2,0:T(8,128)(2,1)S(1)}, u32[]{:S(2)}, u32[]{:S(2)}) collective-permute-start(bf16[4,4,384]{1,2,0:T(8,128)(2,1)S(1)} %get-tuple-element.36), channel_id=1, source_target_pairs={{0,15},{1,0},{2,1},{3,2},{4,3},{5,4},{6,5},{7,6},{8,7},{9,8},{10,9... | collective-permute-start | bytes 36872 | tf_op jit(solution)/shard_map/ppermute | solution.py:10
  11.3 9.0 %collective-permute-done = bf16[4,4,384]{1,2,0:T(8,128)(2,1)S(1)} collective-permute-done((bf16[4,4,384]{1,2,0:T(8,128)(2,1)S(1)}, bf16[4,4,384]{1,2,0:T(8,128)(2,1)S(1)}, u32[]{:S(2)}, u32[]{:S(2)}) %collective-permute-start) | collective-permute-done | bytes 12320 | tf_op jit(solution)/shard_map/ppermute | solution.py:9
  23.0 2.4 %collective-permute-start.2 = (bf16[4,136,384]{2,1,0:T(8,128)(2,1)S(1)}, bf16[4,136,384]{2,1,0:T(8,128)(2,1)}, u32[]{:S(2)}, u32[]{:S(2)}) collective-permute-start(bf16[4,136,384]{2,1,0:T(8,128)(2,1)S(1)} %copy.46), channel_id=1, source_target_pairs={{0,16},{16,32},{32,48},{48,64},{64,80},{80,96},{96,112},{112,128},... | collective-permute-start | bytes 1253384 | tf_op jit(solution)/shard_map/ppermute | solution.py:12
  25.6 5.3 %collective-permute-done.3 = bf16[4,136,384]{2,1,0:T(8,128)(2,1)} collective-permute-done((bf16[4,136,384]{2,1,0:T(8,128)(2,1)S(1)}, bf16[4,136,384]{2,1,0:T(8,128)(2,1)}, u32[]{:S(2)}, u32[]{:S(2)}) %collective-permute-start.3) | collective-permute-done | bytes 417824 | tf_op jit(solution)/shard_map/ppermute | solution.py:13
  32.1 2.6 %collective-permute-done.2 = bf16[4,136,384]{2,1,0:T(8,128)(2,1)} collective-permute-done((bf16[4,136,384]{2,1,0:T(8,128)(2,1)S(1)}, bf16[4,136,384]{2,1,0:T(8,128)(2,1)}, u32[]{:S(2)}, u32[]{:S(2)}) %collective-permute-start.2) | collective-permute-done | bytes 417824 | tf_op jit(solution)/shard_map/ppermute | solution.py:12
  36.9 2.4 %maximum_bitcast_fusion = bf16[10,1,134,192]{2,3,0,1:T(8,128)(2,1)} fusion(bf16[4,136,384]{1,2,0:T(8,128)(2,1)S(1)} %copy.49, bf16[4,136,384]{1,2,0:T(8,128)(2,1)} %copy.48, bf16[4,4,384]{1,2,0:T(8,128)(2,1)S(1)} %collective-permute-done.1, bf16[4,128,384]{1,2,0:T(8,128)(2,1)S(1)} %constant_dynamic-update-slice_fusion, ...), kind=kLoop, calls=%fused_computation.140 | loop fusion | flops 2572800 | bytes 1767936 | tf_op jit(solution)/shard_map/broadcast_in_dim | solution.py:52
  39.3 2.5 %copy.107 = bf16[10,1,134,192]{3,2,0,1:T(8,128)(2,1)} copy(bf16[10,1,134,192]{2,3,0,1:T(8,128)(2,1)} %maximum_bitcast_fusion) | data formatting | bytes 1029120
  68.1 3.0 %copy.103 = f32[8,1,132,192]{2,3,0,1:T(8,128)} copy(f32[8,1,132,192]{3,0,2,1:T(8,128)} %slice.205) | data formatting | bytes 1622016
  78.9 3.1 %copy.104 = f32[8,1,132,192]{2,3,0,1:T(8,128)} copy(f32[8,1,132,192]{3,0,2,1:T(8,128)} %slice.193) | data formatting | bytes 1622016
  82.0 3.0 %reshape.76 = f32[10,1,136,192]{3,2,0,1:T(8,128)} reshape(f32[10,8,17,192]{3,2,1,0:T(8,128)} %copy.64) | data formatting | bytes 2088960 | tf_op jit(solution)/shard_map/conv_general_dilated | solution.py:42
  85.0 2.8 %copy.101 = f32[10,1,134,192]{2,3,0,1:T(8,128)} copy(f32[10,1,134,192]{3,2,0,1:T(8,128)} %bitcast.501) | data formatting | bytes 2058240
  87.8 3.1 %fusion.98 = bf16[10,134,192]{1,2,0:T(8,128)(2,1)} fusion(pred[10]{0:T(512)(128)(4,1)S(1)} %compare_and_fusion.1, f32[10,1,134,192]{2,3,0,1:T(8,128)} %copy.101), kind=kLoop, calls=%fused_computation.141 | loop fusion | flops 1543680 | bytes 1543690 | tf_op jit(solution)/shard_map/jit(_where)/select_n | solution.py:21
  98.5 2.8 %copy.72 = f32[192,9,192]{2,1,0:T(8,128)} copy(f32[192,9,192]{2,0,1:T(8,128)S(1)} %fusion.67) | data formatting | bytes 2654208 | tf_op jit(solution)/shard_map/stack | solution.py:89
  101.2 2.8 %reshape_reshape.9 = f32[2,2,2,2,20736]{4,3,2,1,0:T(2,128)S(1)} reshape(f32[192,9,192]{2,1,0:T(8,128)} %copy.72) | data formatting | bytes 2654208 | tf_op jit(solution)/shard_map/reshape;reshape | solution.py:61
  114.8 4.3 %copy.78 = f32[192,9,192]{2,1,0:T(8,128)} copy(f32[192,9,192]{0,2,1:T(8,128)} %fusion.13) | data formatting | bytes 2654208 | tf_op jit(solution)/shard_map/stack | solution.py:89
  119.2 2.8 %reshape_reshape.11 = f32[2,2,2,2,20736]{4,3,2,1,0:T(2,128)S(1)} reshape(f32[192,9,192]{2,1,0:T(8,128)} %copy.78) | data formatting | bytes 2654208 | tf_op jit(solution)/shard_map/reshape;reshape | solution.py:61
  127.2 2.8 %copy.76 = f32[192,9,192]{2,1,0:T(8,128)} copy(f32[192,9,192]{2,0,1:T(8,128)S(1)} %fusion.40) | data formatting | bytes 2654208 | tf_op jit(solution)/shard_map/stack | solution.py:89
  130.0 3.7 %reshape_reshape.10 = f32[2,2,2,2,20736]{4,3,2,1,0:T(2,128)} reshape(f32[192,9,192]{2,1,0:T(8,128)} %copy.76) | data formatting | bytes 2654208 | tf_op jit(solution)/shard_map/reshape;reshape | solution.py:61
  133.6 4.4 %constant_dynamic-slice_fusion.4 = (f32[2,2,2,1,20736]{4,3,2,1,0:T(1,128)S(1)}, f32[1,2,2,2,20736]{4,0,1,2,3:T(1,128)S(1)}, f32[1,2,2,2,20736]{4,0,1,2,3:T(1,128)S(1)}, f32[2,2,2,1,20736]{4,3,2,1,0:T(1,128)S(1)}) fusion(f32[2,2,2,2,20736]{4,3,2,1,0:T(2,128)S(1)} %reshape_reshape.11, s32[]{:T(128)S(6)} %select_n.69, s32[]{:T(128)S(6)} %select_n.70, ...), kind=kLoop, calls=%fused_computation.301 | loop fusion | bytes 5308424 | tf_op jit(solution)/shard_map/dynamic-slice.4
  147.8 5.0 %collective-permute-done.5 = f32[2,2,20736]{2,0,1:T(2,128)S(1)} collective-permute-done((f32[2,2,20736]{2,0,1:T(2,128)S(1)}, f32[2,2,20736]{2,0,1:T(2,128)S(1)}, u32[]{:S(2)}, u32[]{:S(2)}) %collective-permute-start.5) | collective-permute-done | bytes 331808 | tf_op jit(solution)/shard_map/ppermute | solution.py:67
  153.9 5.9 %collective-permute-done.13 = f32[2,2,20736]{2,0,1:T(2,128)S(1)} collective-permute-done((f32[2,2,20736]{2,0,1:T(2,128)S(1)}, f32[2,2,20736]{2,0,1:T(2,128)S(1)}, u32[]{:S(2)}, u32[]{:S(2)}) %collective-permute-start.13) | collective-permute-done | bytes 331808 | tf_op jit(solution)/shard_map/ppermute | solution.py:67
  161.1 5.4 %collective-permute-done.21 = f32[2,2,20736]{2,0,1:T(2,128)S(1)} collective-permute-done((f32[2,2,20736]{2,0,1:T(2,128)S(1)}, f32[2,2,20736]{2,0,1:T(2,128)S(1)}, u32[]{:S(2)}, u32[]{:S(2)}) %collective-permute-start.21) | collective-permute-done | bytes 331808 | tf_op jit(solution)/shard_map/ppermute | solution.py:67
  169.4 3.1 %collective-permute-start.15 = (f32[20736]{0:T(1024)S(1)}, f32[20736]{0:T(1024)S(1)}, u32[]{:S(2)}, u32[]{:S(2)}) collective-permute-start(f32[20736]{0:T(1024)S(1)} %get-tuple-element.17), channel_id=1, source_target_pairs={{0,128},{16,144},{32,160},{48,176},{64,192},{80,208},{96,224},{112... | collective-permute-start | bytes 248840 | tf_op jit(solution)/shard_map/ppermute | solution.py:67
  177.7 2.8 %collective-permute-done.23 = f32[20736]{0:T(1024)S(1)} collective-permute-done((f32[20736]{0:T(1024)S(1)}, f32[20736]{0:T(1024)S(1)}, u32[]{:S(2)}, u32[]{:S(2)}) %collective-permute-start.23) | collective-permute-done | bytes 82976 | tf_op jit(solution)/shard_map/ppermute | solution.py:67
  183.3 3.3 %collective-permute-start.9 = (f32[20736]{0:T(1024)S(1)}, f32[20736]{0:T(1024)S(1)}, u32[]{:S(2)}, u32[]{:S(2)}) collective-permute-start(f32[20736]{0:T(1024)S(1)} %add.221), channel_id=1, source_target_pairs={{0,2},{1,3},{2,0},{3,1},{4,6},{5,7},{6,4},{7,5},{8,10},{9,11},{10,... | collective-permute-start | bytes 248840 | tf_op jit(solution)/shard_map/ppermute | solution.py:74
  186.7 3.0 %collective-permute-start.25 = (f32[20736]{0:T(1024)S(1)}, f32[20736]{0:T(1024)S(1)}, u32[]{:S(2)}, u32[]{:S(2)}) collective-permute-start(f32[20736]{0:T(1024)S(1)} %add.242), channel_id=1, source_target_pairs={{0,2},{1,3},{2,0},{3,1},{4,6},{5,7},{6,4},{7,5},{8,10},{9,11},{10,... | collective-permute-start | bytes 248840 | tf_op jit(solution)/shard_map/ppermute | solution.py:74
  190.8 3.1 %collective-permute-done.9 = f32[20736]{0:T(1024)S(1)} collective-permute-done((f32[20736]{0:T(1024)S(1)}, f32[20736]{0:T(1024)S(1)}, u32[]{:S(2)}, u32[]{:S(2)}) %collective-permute-start.9) | collective-permute-done | bytes 82976 | tf_op jit(solution)/shard_map/ppermute | solution.py:74
  193.9 6.1 %collective-permute-start.10 = (f32[20736]{0:T(1024)S(1)}, f32[20736]{0:T(1024)S(1)}, u32[]{:S(2)}, u32[]{:S(2)}) collective-permute-start(f32[20736]{0:T(1024)S(1)} %add.222), channel_id=1, source_target_pairs={{0,4},{1,5},{2,6},{3,7},{4,0},{5,1},{6,2},{7,3},{8,12},{9,13},{10,... | collective-permute-start | bytes 248840 | tf_op jit(solution)/shard_map/ppermute | solution.py:74
  200.0 5.0 %collective-permute-start.18 = (f32[20736]{0:T(1024)S(1)}, f32[20736]{0:T(1024)S(1)}, u32[]{:S(2)}, u32[]{:S(2)}) collective-permute-start(f32[20736]{0:T(1024)S(1)} %add.235), channel_id=1, source_target_pairs={{0,4},{1,5},{2,6},{3,7},{4,0},{5,1},{6,2},{7,3},{8,12},{9,13},{10,... | collective-permute-start | bytes 248840 | tf_op jit(solution)/shard_map/ppermute | solution.py:74
  205.0 2.5 %collective-permute-start.26 = (f32[20736]{0:T(1024)S(1)}, f32[20736]{0:T(1024)S(1)}, u32[]{:S(2)}, u32[]{:S(2)}) collective-permute-start(f32[20736]{0:T(1024)S(1)} %add.243), channel_id=1, source_target_pairs={{0,4},{1,5},{2,6},{3,7},{4,0},{5,1},{6,2},{7,3},{8,12},{9,13},{10,... | collective-permute-start | bytes 248840 | tf_op jit(solution)/shard_map/ppermute | solution.py:74
  207.9 2.9 %collective-permute-start.11 = (f32[20736]{0:T(1024)S(1)}, f32[20736]{0:T(1024)S(1)}, u32[]{:S(2)}, u32[]{:S(2)}) collective-permute-start(f32[20736]{0:T(1024)S(1)} %add.223), channel_id=1, source_target_pairs={{0,8},{1,9},{2,10},{3,11},{4,12},{5,13},{6,14},{7,15},{8,0},{9,1},... | collective-permute-start | bytes 248840 | tf_op jit(solution)/shard_map/ppermute | solution.py:74
  213.6 3.0 %collective-permute-start.27 = (f32[20736]{0:T(1024)S(1)}, f32[20736]{0:T(1024)S(1)}, u32[]{:S(2)}, u32[]{:S(2)}) collective-permute-start(f32[20736]{0:T(1024)S(1)} %add.244), channel_id=1, source_target_pairs={{0,8},{1,9},{2,10},{3,11},{4,12},{5,13},{6,14},{7,15},{8,0},{9,1},... | collective-permute-start | bytes 248840 | tf_op jit(solution)/shard_map/ppermute | solution.py:74
  (210 shorter events, 99.3 us)
Async XLA Ops:
  0.6 61.4 %copy-start = (bf16[9,192,192]{2,1,0:T(8,128)(2,1)S(1)}, bf16[9,192,192]{2,1,0:T(8,128)(2,1)}, u32[]{:S(2)}) copy-start(bf16[9,192,192]{2,1,0:T(8,128)(2,1)} %param.7) | copy-start | bytes 1990660
  2.8 17.5 %collective-permute-start = (bf16[4,4,384]{1,2,0:T(8,128)(2,1)S(1)}, bf16[4,4,384]{1,2,0:T(8,128)(2,1)S(1)}, u32[]{:S(2)}, u32[]{:S(2)}) collective-permute-start(bf16[4,4,384]{1,2,0:T(8,128)(2,1)S(1)} %get-tuple-element.35), channel_id=1, source_target_pairs={{0,1},{1,2},{2,3},{3,4},{4,5},{5,6},{6,7},{7,8},{8,9},{9,10},{10,1... | collective-permute-start | bytes 36872 | tf_op jit(solution)/shard_map/ppermute | solution.py:9
  4.8 15.5 %collective-permute-start.1 = (bf16[4,4,384]{1,2,0:T(8,128)(2,1)S(1)}, bf16[4,4,384]{1,2,0:T(8,128)(2,1)S(1)}, u32[]{:S(2)}, u32[]{:S(2)}) collective-permute-start(bf16[4,4,384]{1,2,0:T(8,128)(2,1)S(1)} %get-tuple-element.36), channel_id=1, source_target_pairs={{0,15},{1,0},{2,1},{3,2},{4,3},{5,4},{6,5},{7,6},{8,7},{9,8},{10,9... | collective-permute-start | bytes 36872 | tf_op jit(solution)/shard_map/ppermute | solution.py:10
  21.1 9.7 %collective-permute-start.3 = (bf16[4,136,384]{2,1,0:T(8,128)(2,1)S(1)}, bf16[4,136,384]{2,1,0:T(8,128)(2,1)}, u32[]{:S(2)}, u32[]{:S(2)}) collective-permute-start(bf16[4,136,384]{2,1,0:T(8,128)(2,1)S(1)} %copy.46), channel_id=1, source_target_pairs={{16,0},{32,16},{48,32},{64,48},{80,64},{96,80},{112,96},{128,112},... | collective-permute-start | bytes 1253384 | tf_op jit(solution)/shard_map/ppermute | solution.py:13
  23.0 11.6 %collective-permute-start.2 = (bf16[4,136,384]{2,1,0:T(8,128)(2,1)S(1)}, bf16[4,136,384]{2,1,0:T(8,128)(2,1)}, u32[]{:S(2)}, u32[]{:S(2)}) collective-permute-start(bf16[4,136,384]{2,1,0:T(8,128)(2,1)S(1)} %copy.46), channel_id=1, source_target_pairs={{0,16},{16,32},{32,48},{48,64},{64,80},{80,96},{96,112},{112,128},... | collective-permute-start | bytes 1253384 | tf_op jit(solution)/shard_map/ppermute | solution.py:12
  106.5 33.0 %collective-permute-start.4 = (f32[2,2,2,20736]{3,0,1,2:T(2,128)}, f32[2,2,2,20736]{3,0,1,2:T(2,128)}, u32[]{:S(2)}, u32[]{:S(2)}) collective-permute-start(f32[2,2,2,20736]{3,0,1,2:T(2,128)} %bitcast.485), channel_id=1, source_target_pairs={{0,16},{16,0},{32,48},{48,32},{64,80},{80,64},{96,112},{112,96},{1... | collective-permute-start | bytes 1990664 | tf_op jit(solution)/shard_map/ppermute | solution.py:67
  138.8 4.3 %collective-permute-start.12 = (f32[2,2,2,20736]{3,0,1,2:T(2,128)S(1)}, f32[2,2,2,20736]{3,0,1,2:T(2,128)S(1)}, u32[]{:S(2)}, u32[]{:S(2)}) collective-permute-start(f32[2,2,2,20736]{3,0,1,2:T(2,128)S(1)} %bitcast.512), channel_id=1, source_target_pairs={{0,16},{16,0},{32,48},{48,32},{64,80},{80,64},{96,112},{112,96},{1... | collective-permute-start | bytes 1990664 | tf_op jit(solution)/shard_map/ppermute | solution.py:67
  139.4 6.1 %collective-permute-start.20 = (f32[2,2,2,20736]{3,0,1,2:T(2,128)S(1)}, f32[2,2,2,20736]{3,0,1,2:T(2,128)S(1)}, u32[]{:S(2)}, u32[]{:S(2)}) collective-permute-start(f32[2,2,2,20736]{3,0,1,2:T(2,128)S(1)} %bitcast.511), channel_id=1, source_target_pairs={{0,16},{16,0},{32,48},{48,32},{64,80},{80,64},{96,112},{112,96},{1... | collective-permute-start | bytes 1990664 | tf_op jit(solution)/shard_map/ppermute | solution.py:67
  141.8 11.0 %collective-permute-start.5 = (f32[2,2,20736]{2,0,1:T(2,128)S(1)}, f32[2,2,20736]{2,0,1:T(2,128)S(1)}, u32[]{:S(2)}, u32[]{:S(2)}) collective-permute-start(f32[2,2,20736]{2,0,1:T(2,128)S(1)} %bitcast.514), channel_id=1, source_target_pairs={{0,32},{16,48},{32,0},{48,16},{64,96},{80,112},{96,64},{112,80},{1... | collective-permute-start | bytes 995336 | tf_op jit(solution)/shard_map/ppermute | solution.py:67
  144.3 15.6 %collective-permute-start.13 = (f32[2,2,20736]{2,0,1:T(2,128)S(1)}, f32[2,2,20736]{2,0,1:T(2,128)S(1)}, u32[]{:S(2)}, u32[]{:S(2)}) collective-permute-start(f32[2,2,20736]{2,0,1:T(2,128)S(1)} %bitcast.513), channel_id=1, source_target_pairs={{0,32},{16,48},{32,0},{48,16},{64,96},{80,112},{96,64},{112,80},{1... | collective-permute-start | bytes 995336 | tf_op jit(solution)/shard_map/ppermute | solution.py:67
  146.7 19.7 %collective-permute-start.21 = (f32[2,2,20736]{2,0,1:T(2,128)S(1)}, f32[2,2,20736]{2,0,1:T(2,128)S(1)}, u32[]{:S(2)}, u32[]{:S(2)}) collective-permute-start(f32[2,2,20736]{2,0,1:T(2,128)S(1)} %bitcast.515), channel_id=1, source_target_pairs={{0,32},{16,48},{32,0},{48,16},{64,96},{80,112},{96,64},{112,80},{1... | collective-permute-start | bytes 995336 | tf_op jit(solution)/shard_map/ppermute | solution.py:67
  153.4 14.2 %collective-permute-start.6 = (f32[2,20736]{1,0:T(2,128)S(1)}, f32[2,20736]{1,0:T(2,128)S(1)}, u32[]{:S(2)}, u32[]{:S(2)}) collective-permute-start(f32[2,20736]{1,0:T(2,128)S(1)} %bitcast.516), channel_id=1, source_target_pairs={{0,64},{16,80},{32,96},{48,112},{64,0},{80,16},{96,32},{112,48},{1... | collective-permute-start | bytes 497672 | tf_op jit(solution)/shard_map/ppermute | solution.py:67
  160.5 8.3 %collective-permute-start.14 = (f32[2,20736]{1,0:T(2,128)S(1)}, f32[2,20736]{1,0:T(2,128)S(1)}, u32[]{:S(2)}, u32[]{:S(2)}) collective-permute-start(f32[2,20736]{1,0:T(2,128)S(1)} %bitcast.517), channel_id=1, source_target_pairs={{0,64},{16,80},{32,96},{48,112},{64,0},{80,16},{96,32},{112,48},{1... | collective-permute-start | bytes 497672 | tf_op jit(solution)/shard_map/ppermute | solution.py:67
  167.1 6.8 %collective-permute-start.22 = (f32[2,20736]{1,0:T(2,128)S(1)}, f32[2,20736]{1,0:T(2,128)S(1)}, u32[]{:S(2)}, u32[]{:S(2)}) collective-permute-start(f32[2,20736]{1,0:T(2,128)S(1)} %bitcast.518), channel_id=1, source_target_pairs={{0,64},{16,80},{32,96},{48,112},{64,0},{80,16},{96,32},{112,48},{1... | collective-permute-start | bytes 497672 | tf_op jit(solution)/shard_map/ppermute | solution.py:67
  168.2 7.0 %collective-permute-start.7 = (f32[20736]{0:T(1024)S(1)}, f32[20736]{0:T(1024)S(1)}, u32[]{:S(2)}, u32[]{:S(2)}) collective-permute-start(f32[20736]{0:T(1024)S(1)} %get-tuple-element.19), channel_id=1, source_target_pairs={{0,128},{16,144},{32,160},{48,176},{64,192},{80,208},{96,224},{112... | collective-permute-start | bytes 248840 | tf_op jit(solution)/shard_map/ppermute | solution.py:67
  169.4 6.3 %collective-permute-start.15 = (f32[20736]{0:T(1024)S(1)}, f32[20736]{0:T(1024)S(1)}, u32[]{:S(2)}, u32[]{:S(2)}) collective-permute-start(f32[20736]{0:T(1024)S(1)} %get-tuple-element.17), channel_id=1, source_target_pairs={{0,128},{16,144},{32,160},{48,176},{64,192},{80,208},{96,224},{112... | collective-permute-start | bytes 248840 | tf_op jit(solution)/shard_map/ppermute | solution.py:67
  174.5 6.1 %collective-permute-start.23 = (f32[20736]{0:T(1024)S(1)}, f32[20736]{0:T(1024)S(1)}, u32[]{:S(2)}, u32[]{:S(2)}) collective-permute-start(f32[20736]{0:T(1024)S(1)} %get-tuple-element.15), channel_id=1, source_target_pairs={{0,128},{16,144},{32,160},{48,176},{64,192},{80,208},{96,224},{112... | collective-permute-start | bytes 248840 | tf_op jit(solution)/shard_map/ppermute | solution.py:67
  174.9 5.8 %copy-start.18 = (pred[8,17]{0,1:T(8,128)(4,1)S(1)}, pred[8,17]{0,1:T(8,128)(4,1)}, u32[]{:S(2)}) copy-start(pred[8,17]{0,1:T(8,128)(4,1)} %constant.135) | copy-start | bytes 412
  175.3 8.0 %collective-permute-start.8 = (f32[20736]{0:T(1024)S(1)}, f32[20736]{0:T(1024)S(1)}, u32[]{:S(2)}, u32[]{:S(2)}) collective-permute-start(f32[20736]{0:T(1024)S(1)} %add.220), channel_id=1, source_target_pairs={{0,1},{1,0},{2,3},{3,2},{4,5},{5,4},{6,7},{7,6},{8,9},{9,8},{10,11... | collective-permute-start | bytes 248840 | tf_op jit(solution)/shard_map/ppermute | solution.py:74
  175.8 10.8 %collective-permute-start.16 = (f32[20736]{0:T(1024)S(1)}, f32[20736]{0:T(1024)S(1)}, u32[]{:S(2)}, u32[]{:S(2)}) collective-permute-start(f32[20736]{0:T(1024)S(1)} %add.233), channel_id=1, source_target_pairs={{0,1},{1,0},{2,3},{3,2},{4,5},{5,4},{6,7},{7,6},{8,9},{9,8},{10,11... | collective-permute-start | bytes 248840 | tf_op jit(solution)/shard_map/ppermute | solution.py:74
  180.6 6.2 %collective-permute-start.24 = (f32[20736]{0:T(1024)S(1)}, f32[20736]{0:T(1024)S(1)}, u32[]{:S(2)}, u32[]{:S(2)}) collective-permute-start(f32[20736]{0:T(1024)S(1)} %add.241), channel_id=1, source_target_pairs={{0,1},{1,0},{2,3},{3,2},{4,5},{5,4},{6,7},{7,6},{8,9},{9,8},{10,11... | collective-permute-start | bytes 248840 | tf_op jit(solution)/shard_map/ppermute | solution.py:74
  182.8 6.9 %copy-start.17 = (bf16[9,192,192]{2,1,0:T(8,128)(2,1)S(1)}, bf16[9,192,192]{2,1,0:T(8,128)(2,1)}, u32[]{:S(2)}) copy-start(bf16[9,192,192]{2,1,0:T(8,128)(2,1)} %param.6) | copy-start | bytes 1990660
  183.3 10.7 %collective-permute-start.9 = (f32[20736]{0:T(1024)S(1)}, f32[20736]{0:T(1024)S(1)}, u32[]{:S(2)}, u32[]{:S(2)}) collective-permute-start(f32[20736]{0:T(1024)S(1)} %add.221), channel_id=1, source_target_pairs={{0,2},{1,3},{2,0},{3,1},{4,6},{5,7},{6,4},{7,5},{8,10},{9,11},{10,... | collective-permute-start | bytes 248840 | tf_op jit(solution)/shard_map/ppermute | solution.py:74
  186.6 13.4 %collective-permute-start.17 = (f32[20736]{0:T(1024)S(1)}, f32[20736]{0:T(1024)S(1)}, u32[]{:S(2)}, u32[]{:S(2)}) collective-permute-start(f32[20736]{0:T(1024)S(1)} %add.234), channel_id=1, source_target_pairs={{0,2},{1,3},{2,0},{3,1},{4,6},{5,7},{6,4},{7,5},{8,10},{9,11},{10,... | collective-permute-start | bytes 248840 | tf_op jit(solution)/shard_map/ppermute | solution.py:74
  186.7 18.3 %collective-permute-start.25 = (f32[20736]{0:T(1024)S(1)}, f32[20736]{0:T(1024)S(1)}, u32[]{:S(2)}, u32[]{:S(2)}) collective-permute-start(f32[20736]{0:T(1024)S(1)} %add.242), channel_id=1, source_target_pairs={{0,2},{1,3},{2,0},{3,1},{4,6},{5,7},{6,4},{7,5},{8,10},{9,11},{10,... | collective-permute-start | bytes 248840 | tf_op jit(solution)/shard_map/ppermute | solution.py:74
  193.9 13.9 %collective-permute-start.10 = (f32[20736]{0:T(1024)S(1)}, f32[20736]{0:T(1024)S(1)}, u32[]{:S(2)}, u32[]{:S(2)}) collective-permute-start(f32[20736]{0:T(1024)S(1)} %add.222), channel_id=1, source_target_pairs={{0,4},{1,5},{2,6},{3,7},{4,0},{5,1},{6,2},{7,3},{8,12},{9,13},{10,... | collective-permute-start | bytes 248840 | tf_op jit(solution)/shard_map/ppermute | solution.py:74
  200.0 10.7 %collective-permute-start.18 = (f32[20736]{0:T(1024)S(1)}, f32[20736]{0:T(1024)S(1)}, u32[]{:S(2)}, u32[]{:S(2)}) collective-permute-start(f32[20736]{0:T(1024)S(1)} %add.235), channel_id=1, source_target_pairs={{0,4},{1,5},{2,6},{3,7},{4,0},{5,1},{6,2},{7,3},{8,12},{9,13},{10,... | collective-permute-start | bytes 248840 | tf_op jit(solution)/shard_map/ppermute | solution.py:74
  205.0 8.5 %collective-permute-start.26 = (f32[20736]{0:T(1024)S(1)}, f32[20736]{0:T(1024)S(1)}, u32[]{:S(2)}, u32[]{:S(2)}) collective-permute-start(f32[20736]{0:T(1024)S(1)} %add.243), channel_id=1, source_target_pairs={{0,4},{1,5},{2,6},{3,7},{4,0},{5,1},{6,2},{7,3},{8,12},{9,13},{10,... | collective-permute-start | bytes 248840 | tf_op jit(solution)/shard_map/ppermute | solution.py:74
  207.9 10.7 %collective-permute-start.11 = (f32[20736]{0:T(1024)S(1)}, f32[20736]{0:T(1024)S(1)}, u32[]{:S(2)}, u32[]{:S(2)}) collective-permute-start(f32[20736]{0:T(1024)S(1)} %add.223), channel_id=1, source_target_pairs={{0,8},{1,9},{2,10},{3,11},{4,12},{5,13},{6,14},{7,15},{8,0},{9,1},... | collective-permute-start | bytes 248840 | tf_op jit(solution)/shard_map/ppermute | solution.py:74
  210.8 8.6 %collective-permute-start.19 = (f32[20736]{0:T(1024)S(1)}, f32[20736]{0:T(1024)S(1)}, u32[]{:S(2)}, u32[]{:S(2)}) collective-permute-start(f32[20736]{0:T(1024)S(1)} %add.236), channel_id=1, source_target_pairs={{0,8},{1,9},{2,10},{3,11},{4,12},{5,13},{6,14},{7,15},{8,0},{9,1},... | collective-permute-start | bytes 248840 | tf_op jit(solution)/shard_map/ppermute | solution.py:74
  213.6 6.7 %collective-permute-start.27 = (f32[20736]{0:T(1024)S(1)}, f32[20736]{0:T(1024)S(1)}, u32[]{:S(2)}, u32[]{:S(2)}) collective-permute-start(f32[20736]{0:T(1024)S(1)} %add.244), channel_id=1, source_target_pairs={{0,8},{1,9},{2,10},{3,11},{4,12},{5,13},{6,14},{7,15},{8,0},{9,1},... | collective-permute-start | bytes 248840 | tf_op jit(solution)/shard_map/ppermute | solution.py:74
  216.6 4.5 %copy-start.1 = (bf16[9,192,192]{2,1,0:T(8,128)(2,1)S(1)}, bf16[9,192,192]{2,1,0:T(8,128)(2,1)}, u32[]{:S(2)}) copy-start(bf16[9,192,192]{2,1,0:T(8,128)(2,1)} %param.7) | copy-start | bytes 1990660
  (15 other events, 31.3 us)
where the time goes:
time: 226 us; the launch traced here: 222 us
  local copies, waits for them, and re-layouts  85.6 us (38%)
  starting transfers between devices  52.2 us (23%)
  waiting for transfers between devices  42 us (19%)
  matrix products  22.6 us (10%)
  other arithmetic  17.2 us (8%)
    ppermute x12, starting transfers between devices, all_sum(): x = x + lax.ppermute(x, axis, [(i, i ^ 1 << b) for i in range(n)])  29.8 us
    unnamed x60, local copies, waits for them, and re-layouts  23.4 us
    ppermute x12, waiting for transfers between devices, halve(): x = keep + lax.ppermute(send, axis, [(i, i ^ 1 << b) for i in range(n)])  20.9 us
    dot_general x27, matrix products, kernel_grad(): jnp.einsum('rci,rco->oi', piece, delta, preferred_element_type=jnp.float32)  14.4 us
    conv_general_dilated x11, local copies, waits for them, and re-layouts, forward_conv(): lax.conv_general_dilated(padded[None], w, (1, 1), 'VALID', dimension_numb...  12.9 us
    another operation x3, local copies, waits for them, and re-layouts, kernel_grad(): local_term = jnp.stack(terms, axis=1)  9.86 us
    ppermute x12, starting transfers between devices, halve(): x = keep + lax.ppermute(send, axis, [(i, i ^ 1 << b) for i in range(n)])  9.59 us
    conv_general_dilated x11, local copies, waits for them, and re-layouts, adjoint_conv(): lax.conv_general_dilated(padded[None], w, (1, 1), 'VALID', dimension_numb...  9.37 us
  transfers between devices with their start and end apart: 28, of which 11 were waited for; matrix products, arithmetic and copies ran while one was open for 23% of the time, Pallas kernels for 0%

commit v1 on v0

--- a/solution.py
+++ b/solution.py
@@ -37,21 +37,27 @@
 
 
 def forward_conv(padded, kernel):
-    taps, n_in, n_out = kernel.shape
-    w = kernel.reshape(3, 3, n_in, n_out)
-    return lax.conv_general_dilated(
-        padded[None], w, (1, 1), "VALID", dimension_numbers=("NHWC", "HWIO", "NHWC"),
-        preferred_element_type=jnp.float32,
-    )[0]
+    out_rows, out_cols = (padded.shape[0] - 2, padded.shape[1] - 2)
+    total = jnp.zeros((out_rows, out_cols, kernel.shape[2]), jnp.float32)
+    for tap in range(9):
+        shift_a, shift_b = divmod(tap, 3)
+        piece = padded[shift_a : shift_a + out_rows, shift_b : shift_b + out_cols]
+        total = total + jnp.einsum(
+            "rci,io->rco", piece, kernel[tap], preferred_element_type=jnp.float32
+        )
+    return total
 
 
 def adjoint_conv(padded, kernel):
-    taps, n_in, n_out = kernel.shape
-    w = kernel.reshape(3, 3, n_in, n_out)[::-1, ::-1].transpose(0, 1, 3, 2)
-    return lax.conv_general_dilated(
-        padded[None], w, (1, 1), "VALID", dimension_numbers=("NHWC", "HWIO", "NHWC"),
-        preferred_element_type=jnp.float32,
-    )[0]
+    out_rows, out_cols = (padded.shape[0] - 2, padded.shape[1] - 2)
+    total = jnp.zeros((out_rows, out_cols, kernel.shape[1]), jnp.float32)
+    for tap in range(9):
+        shift_a, shift_b = divmod(tap, 3)
+        piece = padded[2 - shift_a : 2 - shift_a + out_rows, 2 - shift_b : 2 - shift_b + out_cols]
+        total = total + jnp.einsum(
+            "rco,io->rci", piece, kernel[tap], preferred_element_type=jnp.float32
+        )
+    return total
 
 
 def halve(x, axis):
@@ -89,7 +95,7 @@
     local_term = jnp.stack(terms, axis=1)
     n_out, taps, n_in = local_term.shape
     nlat = lax.axis_size("lat")
-    owned = halve(local_term.reshape(nlat, (n_out // nlat) * taps * n_in), "lat")
+    owned = halve(local_term.reshape(nlat, -1, 128), "lat")
     owned = all_sum(owned, "lon")
     return owned.reshape(n_out // nlat, taps, n_in).transpose(1, 2, 0)
 

time: 226 us -> 175 us (0.77)
  the two profiles are of different devices: /device:TPU:24 before, /device:TPU:112 now
where the time goes in v1:
time: 175 us; the launch traced here: 172 us
  waiting for transfers between devices  49.2 us (28%)
  starting transfers between devices  47.2 us (27%)
  matrix products  38.1 us (22%)
  local copies, waits for them, and re-layouts  32.2 us (18%)
  other arithmetic  3.81 us (2%)
    ppermute x12, waiting for transfers between devices, halve(): x = keep + lax.ppermute(send, axis, [(i, i ^ 1 << b) for i in range(n)])  27.1 us
    ppermute x12, starting transfers between devices, all_sum(): x = x + lax.ppermute(x, axis, [(i, i ^ 1 << b) for i in range(n)])  26.1 us
    dot_general x27, matrix products, kernel_grad(): jnp.einsum('rci,rco->oi', piece, delta, preferred_element_type=jnp.float32)  14.9 us
    dot_general x27, matrix products, adjoint_conv(): jnp.einsum('rco,io->rci', piece, kernel[tap], preferred_element_type=jnp....  11.9 us
    dot_general x27, matrix products, forward_conv(): jnp.einsum('rci,io->rco', piece, kernel[tap], preferred_element_type=jnp....  11.4 us
    ppermute x12, starting transfers between devices, halve(): x = keep + lax.ppermute(send, axis, [(i, i ^ 1 << b) for i in range(n)])  11.1 us
    ppermute x12, waiting for transfers between devices, all_sum(): x = x + lax.ppermute(x, axis, [(i, i ^ 1 << b) for i in range(n)])  11 us
    another operation x3, local copies, waits for them, and re-layouts, kernel_grad(): local_term = jnp.stack(terms, axis=1)  10.1 us
  transfers between devices with their start and end apart: 28, of which 17 were waited for; matrix products, arithmetic and copies ran while one was open for 21% of the time, Pallas kernels for 0%

profile of v1, /device:TPU:112, one launch (start us, length us, event | category | flops | bytes accessed | tf_op | source)
XLA Modules:
  0.0 172.2 jit_solution(879312844577275073)
XLA Ops:
  2.9 3.2 %collective-permute-start = (bf16[4,4,384]{2,1,0:T(4,128)(2,1)S(1)}, bf16[4,4,384]{2,1,0:T(4,128)(2,1)S(1)}, u32[]{:S(2)}, u32[]{:S(2)}) collective-permute-start(bf16[4,4,384]{2,1,0:T(4,128)(2,1)S(1)} %get-tuple-element.15), channel_id=1, source_target_pairs={{0,1},{1,2},{2,3},{3,4},{4,5},{5,6},{6,7},{7,8},{8,9},{9,10},{10,1... | collective-permute-start | bytes 36872 | tf_op jit(solution)/shard_map/ppermute | solution.py:9
  6.1 1.4 collective-permute-done
  7.5 3.5 %collective-permute-done.1 = bf16[4,4,384]{2,1,0:T(4,128)(2,1)S(1)} collective-permute-done((bf16[4,4,384]{2,1,0:T(4,128)(2,1)S(1)}, bf16[4,4,384]{2,1,0:T(4,128)(2,1)S(1)}, u32[]{:S(2)}, u32[]{:S(2)}) %collective-permute-start.1) | collective-permute-done | bytes 12320 | tf_op jit(solution)/shard_map/ppermute | solution.py:10
  11.2 2.1 %collective-permute-start.2 = (bf16[4,136,384]{2,1,0:T(8,128)(2,1)S(1)}, bf16[4,136,384]{2,1,0:T(8,128)(2,1)S(1)}, u32[]{:S(2)}, u32[]{:S(2)}) collective-permute-start(bf16[4,136,384]{2,1,0:T(8,128)(2,1)S(1)} %pad_maximum_fusion.1), channel_id=1, source_target_pairs={{0,16},{16,32},{32,48},{48,64},{64,80},{80,96},{96,112},{112,128},... | collective-permute-start | bytes 1253384 | tf_op jit(solution)/shard_map/ppermute | solution.py:12
  13.3 4.7 %collective-permute-start.3 = (bf16[4,136,384]{2,1,0:T(8,128)(2,1)S(1)}, bf16[4,136,384]{2,1,0:T(8,128)(2,1)S(1)}, u32[]{:S(2)}, u32[]{:S(2)}) collective-permute-start(bf16[4,136,384]{2,1,0:T(8,128)(2,1)S(1)} %pad_maximum_fusion.1), channel_id=1, source_target_pairs={{16,0},{32,16},{48,32},{64,48},{80,64},{96,80},{112,96},{128,112},... | collective-permute-start | bytes 1253384 | tf_op jit(solution)/shard_map/ppermute | solution.py:13
  18.1 5.3 %collective-permute-done.2 = bf16[4,136,384]{2,1,0:T(8,128)(2,1)S(1)} collective-permute-done((bf16[4,136,384]{2,1,0:T(8,128)(2,1)S(1)}, bf16[4,136,384]{2,1,0:T(8,128)(2,1)S(1)}, u32[]{:S(2)}, u32[]{:S(2)}) %collective-permute-start.2) | collective-permute-done | bytes 417824 | tf_op jit(solution)/shard_map/ppermute | solution.py:12
  31.3 2.0 %fusion.126 = (bf16[10,134,192]{2,1,0:T(8,128)(2,1)S(1)}, f32[10,134,192]{2,1,0:T(8,128)}) fusion(pred[10]{0:T(512)(128)(4,1)S(1)} %compare_and_fusion.1, f32[10,134,192]{2,1,0:T(8,128)S(1)} %fusion.109, f32[10,134,192]{2,1,0:T(8,128)S(1)} %fusion.111, f32[10,134,192]{2,1,0:T(8,128)S(1)} %fusion.113, f32[10,134,192]{2,1,0:T(8,128)S(1)} %fusion.115, ...), kind=kOutput, calls=%fused_computation.192 | convolution fusion | flops 102397440 | bytes 13479936 | tf_op jit(solution)/shard_map/rci,io->rco/dot_general | solution.py:45
  49.0 4.4 %copy.274 = f32[192,9,192]{2,1,0:T(8,128)} copy(f32[192,9,192]{0,2,1:T(8,128)} %fusion.21) | data formatting | bytes 2654208 | tf_op jit(solution)/shard_map/stack | solution.py:95
  53.5 2.4 %reshape_reshape.11 = f32[2,2,2,2,162,128]{5,4,3,2,1,0:T(8,128)S(1)} reshape(f32[192,9,192]{2,1,0:T(8,128)} %copy.274) | data formatting | bytes 2654208 | tf_op jit(solution)/shard_map/reshape;reshape | solution.py:67
  57.3 1.5 collective-permute-start.20
  61.4 2.8 %copy.262 = f32[192,9,192]{2,1,0:T(8,128)} copy(f32[192,9,192]{2,0,1:T(8,128)S(1)} %fusion.48) | data formatting | bytes 2654208 | tf_op jit(solution)/shard_map/stack | solution.py:95
  64.2 3.3 %reshape_reshape.10 = f32[2,2,2,2,162,128]{5,4,3,2,1,0:T(8,128)} reshape(f32[192,9,192]{2,1,0:T(8,128)} %copy.262) | data formatting | bytes 2654208 | tf_op jit(solution)/shard_map/reshape;reshape | solution.py:67
  68.7 1.4 copy.263
  79.1 2.9 %copy.241 = f32[192,9,192]{2,1,0:T(8,128)} copy(f32[192,9,192]{2,0,1:T(8,128)S(1)} %fusion.75) | data formatting | bytes 2654208 | tf_op jit(solution)/shard_map/stack | solution.py:95
  82.0 3.3 %reshape_reshape.9 = f32[2,2,2,2,162,128]{5,4,3,2,1,0:T(8,128)} reshape(f32[192,9,192]{2,1,0:T(8,128)} %copy.241) | data formatting | bytes 2654208 | tf_op jit(solution)/shard_map/reshape;reshape | solution.py:67
  92.9 1.6 collective-permute-start.21
  96.5 1.6 collective-permute-start.5
  98.1 5.9 %collective-permute-done.21 = f32[2,2,162,128]{3,2,0,1:T(8,128)S(1)} collective-permute-done((f32[2,2,162,128]{3,2,0,1:T(8,128)S(1)}, f32[2,2,162,128]{3,2,0,1:T(8,128)S(1)}, u32[]{:S(2)}, u32[]{:S(2)}) %collective-permute-start.21) | collective-permute-done | bytes 331808 | tf_op jit(solution)/shard_map/ppermute | solution.py:73
  104.3 7.0 %collective-permute-done.13 = f32[2,2,162,128]{3,2,0,1:T(8,128)S(1)} collective-permute-done((f32[2,2,162,128]{3,2,0,1:T(8,128)S(1)}, f32[2,2,162,128]{3,2,0,1:T(8,128)S(1)}, u32[]{:S(2)}, u32[]{:S(2)}) %collective-permute-start.13) | collective-permute-done | bytes 331808 | tf_op jit(solution)/shard_map/ppermute | solution.py:73
  111.5 6.3 %collective-permute-done.5 = f32[2,2,162,128]{3,2,0,1:T(8,128)S(1)} collective-permute-done((f32[2,2,162,128]{3,2,0,1:T(8,128)S(1)}, f32[2,2,162,128]{3,2,0,1:T(8,128)S(1)}, u32[]{:S(2)}, u32[]{:S(2)}) %collective-permute-start.5) | collective-permute-done | bytes 331808 | tf_op jit(solution)/shard_map/ppermute | solution.py:73
  118.2 2.1 %collective-permute-start.23 = (f32[162,128]{1,0:T(8,128)S(1)}, f32[162,128]{1,0:T(8,128)S(1)}, u32[]{:S(2)}, u32[]{:S(2)}) collective-permute-start(f32[162,128]{1,0:T(8,128)S(1)} %dynamic-slice_bitcast_fusion.9), channel_id=1, source_target_pairs={{0,128},{16,144},{32,160},{48,176},{64,192},{80,208},{96,224},{112... | collective-permute-start | bytes 248840 | tf_op jit(solution)/shard_map/ppermute | solution.py:73
  120.3 1.6 collective-permute-start.15
  121.9 3.2 %collective-permute-done.6 = f32[2,162,128]{2,1,0:T(8,128)S(1)} collective-permute-done((f32[2,162,128]{2,1,0:T(8,128)S(1)}, f32[2,162,128]{2,1,0:T(8,128)S(1)}, u32[]{:S(2)}, u32[]{:S(2)}) %collective-permute-start.6) | collective-permute-done | bytes 165920 | tf_op jit(solution)/shard_map/ppermute | solution.py:73
  128.9 2.3 %collective-permute-done.7 = f32[162,128]{1,0:T(8,128)S(1)} collective-permute-done((f32[162,128]{1,0:T(8,128)S(1)}, f32[162,128]{1,0:T(8,128)S(1)}, u32[]{:S(2)}, u32[]{:S(2)}) %collective-permute-start.7) | collective-permute-done | bytes 82976 | tf_op jit(solution)/shard_map/ppermute | solution.py:73
  134.1 1.9 %collective-permute-start.17 = (f32[162,128]{1,0:T(8,128)S(1)}, f32[162,128]{1,0:T(8,128)S(1)}, u32[]{:S(2)}, u32[]{:S(2)}) collective-permute-start(f32[162,128]{1,0:T(8,128)S(1)} %add.408), channel_id=1, source_target_pairs={{0,2},{1,3},{2,0},{3,1},{4,6},{5,7},{6,4},{7,5},{8,10},{9,11},{10,... | collective-permute-start | bytes 248840 | tf_op jit(solution)/shard_map/ppermute | solution.py:80
  137.5 6.9 %collective-permute-done.25 = f32[162,128]{1,0:T(8,128)S(1)} collective-permute-done((f32[162,128]{1,0:T(8,128)S(1)}, f32[162,128]{1,0:T(8,128)S(1)}, u32[]{:S(2)}, u32[]{:S(2)}) %collective-permute-start.25) | collective-permute-done | bytes 82976 | tf_op jit(solution)/shard_map/ppermute | solution.py:80
  144.4 6.6 %collective-permute-start.26 = (f32[162,128]{1,0:T(8,128)S(1)}, f32[162,128]{1,0:T(8,128)S(1)}, u32[]{:S(2)}, u32[]{:S(2)}) collective-permute-start(f32[162,128]{1,0:T(8,128)S(1)} %add.417), channel_id=1, source_target_pairs={{0,4},{1,5},{2,6},{3,7},{4,0},{5,1},{6,2},{7,3},{8,12},{9,13},{10,... | collective-permute-start | bytes 248840 | tf_op jit(solution)/shard_map/ppermute | solution.py:80
  151.1 2.1 %collective-permute-start.18 = (f32[162,128]{1,0:T(8,128)S(1)}, f32[162,128]{1,0:T(8,128)S(1)}, u32[]{:S(2)}, u32[]{:S(2)}) collective-permute-start(f32[162,128]{1,0:T(8,128)S(1)} %add.409), channel_id=1, source_target_pairs={{0,4},{1,5},{2,6},{3,7},{4,0},{5,1},{6,2},{7,3},{8,12},{9,13},{10,... | collective-permute-start | bytes 248840 | tf_op jit(solution)/shard_map/ppermute | solution.py:80
  153.2 4.0 %collective-permute-start.10 = (f32[162,128]{1,0:T(8,128)S(1)}, f32[162,128]{1,0:T(8,128)S(1)}, u32[]{:S(2)}, u32[]{:S(2)}) collective-permute-start(f32[162,128]{1,0:T(8,128)S(1)} %add.401), channel_id=1, source_target_pairs={{0,4},{1,5},{2,6},{3,7},{4,0},{5,1},{6,2},{7,3},{8,12},{9,13},{10,... | collective-permute-start | bytes 248840 | tf_op jit(solution)/shard_map/ppermute | solution.py:80
  157.5 5.4 %collective-permute-start.27 = (f32[162,128]{1,0:T(8,128)S(1)}, f32[162,128]{1,0:T(8,128)S(1)}, u32[]{:S(2)}, u32[]{:S(2)}) collective-permute-start(f32[162,128]{1,0:T(8,128)S(1)} %add.418), channel_id=1, source_target_pairs={{0,8},{1,9},{2,10},{3,11},{4,12},{5,13},{6,14},{7,15},{8,0},{9,1},... | collective-permute-start | bytes 248840 | tf_op jit(solution)/shard_map/ppermute | solution.py:80
  162.9 2.2 %collective-permute-start.19 = (f32[162,128]{1,0:T(8,128)S(1)}, f32[162,128]{1,0:T(8,128)S(1)}, u32[]{:S(2)}, u32[]{:S(2)}) collective-permute-start(f32[162,128]{1,0:T(8,128)S(1)} %add.410), channel_id=1, source_target_pairs={{0,8},{1,9},{2,10},{3,11},{4,12},{5,13},{6,14},{7,15},{8,0},{9,1},... | collective-permute-start | bytes 248840 | tf_op jit(solution)/shard_map/ppermute | solution.py:80
  165.1 1.5 collective-permute-start.11
  (205 shorter events, 64.1 us)
Async XLA Ops:
  2.8 21.7 %copy-start.2 = (bf16[4,128,192]{2,1,0:T(8,128)(2,1)}, bf16[4,128,192]{2,1,0:T(8,128)(2,1)S(1)}, u32[]{:S(2)}) copy-start(bf16[4,128,192]{2,1,0:T(8,128)(2,1)S(1)} %copy.187) | copy-start | bytes 589828
  2.9 4.6 %collective-permute-start = (bf16[4,4,384]{2,1,0:T(4,128)(2,1)S(1)}, bf16[4,4,384]{2,1,0:T(4,128)(2,1)S(1)}, u32[]{:S(2)}, u32[]{:S(2)}) collective-permute-start(bf16[4,4,384]{2,1,0:T(4,128)(2,1)S(1)} %get-tuple-element.15), channel_id=1, source_target_pairs={{0,1},{1,2},{2,3},{3,4},{4,5},{5,6},{6,7},{7,8},{8,9},{9,10},{10,1... | collective-permute-start | bytes 36872 | tf_op jit(solution)/shard_map/ppermute | solution.py:9
  6.1 4.9 %collective-permute-start.1 = (bf16[4,4,384]{2,1,0:T(4,128)(2,1)S(1)}, bf16[4,4,384]{2,1,0:T(4,128)(2,1)S(1)}, u32[]{:S(2)}, u32[]{:S(2)}) collective-permute-start(bf16[4,4,384]{2,1,0:T(4,128)(2,1)S(1)} %get-tuple-element.16), channel_id=1, source_target_pairs={{0,15},{1,0},{2,1},{3,2},{4,3},{5,4},{6,5},{7,6},{8,7},{9,8},{10,9... | collective-permute-start | bytes 36872 | tf_op jit(solution)/shard_map/ppermute | solution.py:10
  11.2 13.3 %copy-start.4 = (bf16[9,192,192]{2,1,0:T(8,128)(2,1)S(1)}, bf16[9,192,192]{2,1,0:T(8,128)(2,1)}, u32[]{:S(2)}) copy-start(bf16[9,192,192]{2,1,0:T(8,128)(2,1)} %param.6) | copy-start | bytes 1990660
  11.2 12.2 %collective-permute-start.2 = (bf16[4,136,384]{2,1,0:T(8,128)(2,1)S(1)}, bf16[4,136,384]{2,1,0:T(8,128)(2,1)S(1)}, u32[]{:S(2)}, u32[]{:S(2)}) collective-permute-start(bf16[4,136,384]{2,1,0:T(8,128)(2,1)S(1)} %pad_maximum_fusion.1), channel_id=1, source_target_pairs={{0,16},{16,32},{32,48},{48,64},{64,80},{80,96},{96,112},{112,128},... | collective-permute-start | bytes 1253384 | tf_op jit(solution)/shard_map/ppermute | solution.py:12
  13.3 10.9 %collective-permute-start.3 = (bf16[4,136,384]{2,1,0:T(8,128)(2,1)S(1)}, bf16[4,136,384]{2,1,0:T(8,128)(2,1)S(1)}, u32[]{:S(2)}, u32[]{:S(2)}) collective-permute-start(bf16[4,136,384]{2,1,0:T(8,128)(2,1)S(1)} %pad_maximum_fusion.1), channel_id=1, source_target_pairs={{16,0},{32,16},{48,32},{64,48},{80,64},{96,80},{112,96},{128,112},... | collective-permute-start | bytes 1253384 | tf_op jit(solution)/shard_map/ppermute | solution.py:13
  57.3 34.2 %collective-permute-start.20 = (f32[2,2,2,162,128]{4,2,3,1,0:T(2,128)}, f32[2,2,2,162,128]{4,2,3,1,0:T(2,128)}, u32[]{:S(2)}, u32[]{:S(2)}) collective-permute-start(f32[2,2,2,162,128]{4,2,3,1,0:T(2,128)} %copy.275), channel_id=1, source_target_pairs={{0,16},{16,0},{32,48},{48,32},{64,80},{80,64},{96,112},{112,96},{1... | collective-permute-start | bytes 1990664 | tf_op jit(solution)/shard_map/ppermute | solution.py:73
  67.5 3.1 %copy-start.10 = (bf16[9,192,192]{2,1,0:T(8,128)(2,1)S(1)}, bf16[9,192,192]{2,1,0:T(8,128)(2,1)}, u32[]{:S(2)}) copy-start(bf16[9,192,192]{2,1,0:T(8,128)(2,1)} %param.7) | copy-start | bytes 1990660
  70.1 24.4 %collective-permute-start.12 = (f32[2,2,2,162,128]{4,2,3,1,0:T(2,128)}, f32[2,2,2,162,128]{4,2,3,1,0:T(2,128)}, u32[]{:S(2)}, u32[]{:S(2)}) collective-permute-start(f32[2,2,2,162,128]{4,2,3,1,0:T(2,128)} %copy.263), channel_id=1, source_target_pairs={{0,16},{16,0},{32,48},{48,32},{64,80},{80,64},{96,112},{112,96},{1... | collective-permute-start | bytes 1990664 | tf_op jit(solution)/shard_map/ppermute | solution.py:73
  87.1 9.3 %collective-permute-start.4 = (f32[2,2,2,162,128]{4,2,3,1,0:T(2,128)S(1)}, f32[2,2,2,162,128]{4,2,3,1,0:T(2,128)S(1)}, u32[]{:S(2)}, u32[]{:S(2)}) collective-permute-start(f32[2,2,2,162,128]{4,2,3,1,0:T(2,128)S(1)} %copy.242), channel_id=1, source_target_pairs={{0,16},{16,0},{32,48},{48,32},{64,80},{80,64},{96,112},{112,96},{1... | collective-permute-start | bytes 1990664 | tf_op jit(solution)/shard_map/ppermute | solution.py:73
  92.9 3.5 %copy-start.1 = (f32[2,2,2,2,162,128]{5,4,3,2,1,0:T(8,128)S(1)}, f32[2,2,2,2,162,128]{5,4,3,2,1,0:T(8,128)}, u32[]{:S(2)}) copy-start(f32[2,2,2,2,162,128]{5,4,3,2,1,0:T(8,128)} %reshape_reshape.9) | copy-start | bytes 3981316
  92.9 11.0 %collective-permute-start.21 = (f32[2,2,162,128]{3,2,0,1:T(8,128)S(1)}, f32[2,2,162,128]{3,2,0,1:T(8,128)S(1)}, u32[]{:S(2)}, u32[]{:S(2)}) collective-permute-start(f32[2,2,162,128]{3,2,0,1:T(8,128)S(1)} %dynamic-slice_bitcast_fusion.3), channel_id=1, source_target_pairs={{0,32},{16,48},{32,0},{48,16},{64,96},{80,112},{96,64},{112,80},{1... | collective-permute-start | bytes 995336 | tf_op jit(solution)/shard_map/ppermute | solution.py:73
  95.7 15.6 %collective-permute-start.13 = (f32[2,2,162,128]{3,2,0,1:T(8,128)S(1)}, f32[2,2,162,128]{3,2,0,1:T(8,128)S(1)}, u32[]{:S(2)}, u32[]{:S(2)}) collective-permute-start(f32[2,2,162,128]{3,2,0,1:T(8,128)S(1)} %dynamic-slice_bitcast_fusion.4), channel_id=1, source_target_pairs={{0,32},{16,48},{32,0},{48,16},{64,96},{80,112},{96,64},{112,80},{1... | collective-permute-start | bytes 995336 | tf_op jit(solution)/shard_map/ppermute | solution.py:73
  96.5 21.3 %collective-permute-start.5 = (f32[2,2,162,128]{3,2,0,1:T(8,128)S(1)}, f32[2,2,162,128]{3,2,0,1:T(8,128)S(1)}, u32[]{:S(2)}, u32[]{:S(2)}) collective-permute-start(f32[2,2,162,128]{3,2,0,1:T(8,128)S(1)} %dynamic-slice_bitcast_fusion.5), channel_id=1, source_target_pairs={{0,32},{16,48},{32,0},{48,16},{64,96},{80,112},{96,64},{112,80},{1... | collective-permute-start | bytes 995336 | tf_op jit(solution)/shard_map/ppermute | solution.py:73
  104.0 14.1 %collective-permute-start.22 = (f32[2,162,128]{2,1,0:T(8,128)S(1)}, f32[2,162,128]{2,1,0:T(8,128)S(1)}, u32[]{:S(2)}, u32[]{:S(2)}) collective-permute-start(f32[2,162,128]{2,1,0:T(8,128)S(1)} %dynamic-slice_bitcast_fusion.6), channel_id=1, source_target_pairs={{0,64},{16,80},{32,96},{48,112},{64,0},{80,16},{96,32},{112,48},{1... | collective-permute-start | bytes 497672 | tf_op jit(solution)/shard_map/ppermute | solution.py:73
  111.4 8.9 %collective-permute-start.14 = (f32[2,162,128]{2,1,0:T(8,128)S(1)}, f32[2,162,128]{2,1,0:T(8,128)S(1)}, u32[]{:S(2)}, u32[]{:S(2)}) collective-permute-start(f32[2,162,128]{2,1,0:T(8,128)S(1)} %dynamic-slice_bitcast_fusion.7), channel_id=1, source_target_pairs={{0,64},{16,80},{32,96},{48,112},{64,0},{80,16},{96,32},{112,48},{1... | collective-permute-start | bytes 497672 | tf_op jit(solution)/shard_map/ppermute | solution.py:73
  117.8 7.3 %collective-permute-start.6 = (f32[2,162,128]{2,1,0:T(8,128)S(1)}, f32[2,162,128]{2,1,0:T(8,128)S(1)}, u32[]{:S(2)}, u32[]{:S(2)}) collective-permute-start(f32[2,162,128]{2,1,0:T(8,128)S(1)} %dynamic-slice_bitcast_fusion.8), channel_id=1, source_target_pairs={{0,64},{16,80},{32,96},{48,112},{64,0},{80,16},{96,32},{112,48},{1... | collective-permute-start | bytes 497672 | tf_op jit(solution)/shard_map/ppermute | solution.py:73
  118.2 8.5 %collective-permute-start.23 = (f32[162,128]{1,0:T(8,128)S(1)}, f32[162,128]{1,0:T(8,128)S(1)}, u32[]{:S(2)}, u32[]{:S(2)}) collective-permute-start(f32[162,128]{1,0:T(8,128)S(1)} %dynamic-slice_bitcast_fusion.9), channel_id=1, source_target_pairs={{0,128},{16,144},{32,160},{48,176},{64,192},{80,208},{96,224},{112... | collective-permute-start | bytes 248840 | tf_op jit(solution)/shard_map/ppermute | solution.py:73
  120.3 7.8 %collective-permute-start.15 = (f32[162,128]{1,0:T(8,128)S(1)}, f32[162,128]{1,0:T(8,128)S(1)}, u32[]{:S(2)}, u32[]{:S(2)}) collective-permute-start(f32[162,128]{1,0:T(8,128)S(1)} %dynamic-slice_bitcast_fusion.10), channel_id=1, source_target_pairs={{0,128},{16,144},{32,160},{48,176},{64,192},{80,208},{96,224},{112... | collective-permute-start | bytes 248840 | tf_op jit(solution)/shard_map/ppermute | solution.py:73
  125.2 6.1 %collective-permute-start.7 = (f32[162,128]{1,0:T(8,128)S(1)}, f32[162,128]{1,0:T(8,128)S(1)}, u32[]{:S(2)}, u32[]{:S(2)}) collective-permute-start(f32[162,128]{1,0:T(8,128)S(1)} %dynamic-slice_bitcast_fusion.11), channel_id=1, source_target_pairs={{0,128},{16,144},{32,160},{48,176},{64,192},{80,208},{96,224},{112... | collective-permute-start | bytes 248840 | tf_op jit(solution)/shard_map/ppermute | solution.py:73
  126.7 6.2 %collective-permute-start.24 = (f32[162,128]{1,0:T(8,128)S(1)}, f32[162,128]{1,0:T(8,128)S(1)}, u32[]{:S(2)}, u32[]{:S(2)}) collective-permute-start(f32[162,128]{1,0:T(8,128)S(1)} %bitcast_add_fusion.9), channel_id=1, source_target_pairs={{0,1},{1,0},{2,3},{3,2},{4,5},{5,4},{6,7},{7,6},{8,9},{9,8},{10,11... | collective-permute-start | bytes 248840 | tf_op jit(solution)/shard_map/ppermute | solution.py:80
  128.1 6.0 %collective-permute-start.16 = (f32[162,128]{1,0:T(8,128)S(1)}, f32[162,128]{1,0:T(8,128)S(1)}, u32[]{:S(2)}, u32[]{:S(2)}) collective-permute-start(f32[162,128]{1,0:T(8,128)S(1)} %bitcast_add_fusion.10), channel_id=1, source_target_pairs={{0,1},{1,0},{2,3},{3,2},{4,5},{5,4},{6,7},{7,6},{8,9},{9,8},{10,11... | collective-permute-start | bytes 248840 | tf_op jit(solution)/shard_map/ppermute | solution.py:80
  131.3 5.1 %collective-permute-start.8 = (f32[162,128]{1,0:T(8,128)S(1)}, f32[162,128]{1,0:T(8,128)S(1)}, u32[]{:S(2)}, u32[]{:S(2)}) collective-permute-start(f32[162,128]{1,0:T(8,128)S(1)} %bitcast_add_fusion.11), channel_id=1, source_target_pairs={{0,1},{1,0},{2,3},{3,2},{4,5},{5,4},{6,7},{7,6},{8,9},{9,8},{10,11... | collective-permute-start | bytes 248840 | tf_op jit(solution)/shard_map/ppermute | solution.py:80
  132.9 11.5 %collective-permute-start.25 = (f32[162,128]{1,0:T(8,128)S(1)}, f32[162,128]{1,0:T(8,128)S(1)}, u32[]{:S(2)}, u32[]{:S(2)}) collective-permute-start(f32[162,128]{1,0:T(8,128)S(1)} %add.416), channel_id=1, source_target_pairs={{0,2},{1,3},{2,0},{3,1},{4,6},{5,7},{6,4},{7,5},{8,10},{9,11},{10,... | collective-permute-start | bytes 248840 | tf_op jit(solution)/shard_map/ppermute | solution.py:80
  134.1 16.9 %collective-permute-start.17 = (f32[162,128]{1,0:T(8,128)S(1)}, f32[162,128]{1,0:T(8,128)S(1)}, u32[]{:S(2)}, u32[]{:S(2)}) collective-permute-start(f32[162,128]{1,0:T(8,128)S(1)} %add.408), channel_id=1, source_target_pairs={{0,2},{1,3},{2,0},{3,1},{4,6},{5,7},{6,4},{7,5},{8,10},{9,11},{10,... | collective-permute-start | bytes 248840 | tf_op jit(solution)/shard_map/ppermute | solution.py:80
  136.3 16.8 %collective-permute-start.9 = (f32[162,128]{1,0:T(8,128)S(1)}, f32[162,128]{1,0:T(8,128)S(1)}, u32[]{:S(2)}, u32[]{:S(2)}) collective-permute-start(f32[162,128]{1,0:T(8,128)S(1)} %add.400), channel_id=1, source_target_pairs={{0,2},{1,3},{2,0},{3,1},{4,6},{5,7},{6,4},{7,5},{8,10},{9,11},{10,... | collective-permute-start | bytes 248840 | tf_op jit(solution)/shard_map/ppermute | solution.py:80
  144.4 13.0 %collective-permute-start.26 = (f32[162,128]{1,0:T(8,128)S(1)}, f32[162,128]{1,0:T(8,128)S(1)}, u32[]{:S(2)}, u32[]{:S(2)}) collective-permute-start(f32[162,128]{1,0:T(8,128)S(1)} %add.417), channel_id=1, source_target_pairs={{0,4},{1,5},{2,6},{3,7},{4,0},{5,1},{6,2},{7,3},{8,12},{9,13},{10,... | collective-permute-start | bytes 248840 | tf_op jit(solution)/shard_map/ppermute | solution.py:80
  151.1 11.9 %collective-permute-start.18 = (f32[162,128]{1,0:T(8,128)S(1)}, f32[162,128]{1,0:T(8,128)S(1)}, u32[]{:S(2)}, u32[]{:S(2)}) collective-permute-start(f32[162,128]{1,0:T(8,128)S(1)} %add.409), channel_id=1, source_target_pairs={{0,4},{1,5},{2,6},{3,7},{4,0},{5,1},{6,2},{7,3},{8,12},{9,13},{10,... | collective-permute-start | bytes 248840 | tf_op jit(solution)/shard_map/ppermute | solution.py:80
  153.2 11.9 %collective-permute-start.10 = (f32[162,128]{1,0:T(8,128)S(1)}, f32[162,128]{1,0:T(8,128)S(1)}, u32[]{:S(2)}, u32[]{:S(2)}) collective-permute-start(f32[162,128]{1,0:T(8,128)S(1)} %add.401), channel_id=1, source_target_pairs={{0,4},{1,5},{2,6},{3,7},{4,0},{5,1},{6,2},{7,3},{8,12},{9,13},{10,... | collective-permute-start | bytes 248840 | tf_op jit(solution)/shard_map/ppermute | solution.py:80
  157.5 10.2 %collective-permute-start.27 = (f32[162,128]{1,0:T(8,128)S(1)}, f32[162,128]{1,0:T(8,128)S(1)}, u32[]{:S(2)}, u32[]{:S(2)}) collective-permute-start(f32[162,128]{1,0:T(8,128)S(1)} %add.418), channel_id=1, source_target_pairs={{0,8},{1,9},{2,10},{3,11},{4,12},{5,13},{6,14},{7,15},{8,0},{9,1},... | collective-permute-start | bytes 248840 | tf_op jit(solution)/shard_map/ppermute | solution.py:80
  162.9 6.1 %collective-permute-start.19 = (f32[162,128]{1,0:T(8,128)S(1)}, f32[162,128]{1,0:T(8,128)S(1)}, u32[]{:S(2)}, u32[]{:S(2)}) collective-permute-start(f32[162,128]{1,0:T(8,128)S(1)} %add.410), channel_id=1, source_target_pairs={{0,8},{1,9},{2,10},{3,11},{4,12},{5,13},{6,14},{7,15},{8,0},{9,1},... | collective-permute-start | bytes 248840 | tf_op jit(solution)/shard_map/ppermute | solution.py:80
  165.1 6.1 %collective-permute-start.11 = (f32[162,128]{1,0:T(8,128)S(1)}, f32[162,128]{1,0:T(8,128)S(1)}, u32[]{:S(2)}, u32[]{:S(2)}) collective-permute-start(f32[162,128]{1,0:T(8,128)S(1)} %add.402), channel_id=1, source_target_pairs={{0,8},{1,9},{2,10},{3,11},{4,12},{5,13},{6,14},{7,15},{8,0},{9,1},... | collective-permute-start | bytes 248840 | tf_op jit(solution)/shard_map/ppermute | solution.py:80
  (16 other events, 27.5 us)

commit v2 on v1

--- a/solution.py
+++ b/solution.py
@@ -60,24 +60,44 @@
     return total
 
 
+def gray(n_bits, low):
+    def label(i):
+        ring = (i >> low) & ((1 << n_bits) - 1)
+        return (i & ~(((1 << n_bits) - 1) << low)) | ((ring ^ (ring >> 1)) << low)
+    return label
+
+
+def labels(axis):
+    n = lax.axis_size(axis)
+    label = gray(2, 2) if axis == "lat" else gray(3, 0)
+    lab = [label(i) for i in range(n)]
+    pos = [0] * n
+    for i, l in enumerate(lab):
+        pos[l] = i
+    return lab, pos
+
+
 def halve(x, axis):
     n = lax.axis_size(axis)
     bits = n.bit_length() - 1
-    me = lax.axis_index(axis)
+    lab, pos = labels(axis)
+    x = jnp.stack([x[pos[l]] for l in range(n)])
+    me = jnp.asarray(lab, jnp.int32)[lax.axis_index(axis)]
     x = x.reshape((2,) * bits + x.shape[1:])
     x = x.transpose(tuple(range(bits - 1, -1, -1)) + tuple(range(bits, x.ndim)))
     for b in range(bits):
         mine = (me >> b) & 1
         keep = lax.dynamic_index_in_dim(x, mine, 0, keepdims=False)
         send = lax.dynamic_index_in_dim(x, 1 - mine, 0, keepdims=False)
-        x = keep + lax.ppermute(send, axis, [(i, i ^ (1 << b)) for i in range(n)])
+        x = keep + lax.ppermute(send, axis, [(i, pos[lab[i] ^ (1 << b)]) for i in range(n)])
     return x
 
 
 def all_sum(x, axis):
     n = lax.axis_size(axis)
+    lab, pos = labels(axis)
     for b in range(n.bit_length() - 1):
-        x = x + lax.ppermute(x, axis, [(i, i ^ (1 << b)) for i in range(n)])
+        x = x + lax.ppermute(x, axis, [(i, pos[lab[i] ^ (1 << b)]) for i in range(n)])
     return x
 
 

time: 175 us -> 285 us (1.63)
  the two profiles are of different devices: /device:TPU:112 before, /device:TPU:32 now
where the time goes in v2:
time: 285 us; the launch traced here: 281 us
  local copies, waits for them, and re-layouts  149 us (52%)
  starting transfers between devices  51.4 us (18%)
  matrix products  36.9 us (13%)
  waiting for transfers between devices  34 us (12%)
  between operations  5 us (2%)
  other arithmetic  4.39 us (2%)
    slice x99, local copies, waits for them, and re-layouts, halve(): x = jnp.stack([x[pos[l]] for l in range(n)])  107 us
    unnamed x169, local copies, waits for them, and re-layouts  37.4 us
    ppermute x12, starting transfers between devices, halve(): lax.ppermute(send, axis, [(i, pos[lab[i] ^ 1 << b]) for i in range(n)])  25.5 us
    ppermute x12, starting transfers between devices, all_sum(): x = x + lax.ppermute(x, axis, [(i, pos[lab[i] ^ 1 << b]) for i in range(n)])  19.2 us
    dot_general x27, matrix products, kernel_grad(): jnp.einsum('rci,rco->oi', piece, delta, preferred_element_type=jnp.float32)  14.4 us
    ppermute x12, waiting for transfers between devices, all_sum(): x = x + lax.ppermute(x, axis, [(i, pos[lab[i] ^ 1 << b]) for i in range(n)])  13.3 us
    dot_general x27, matrix products, adjoint_conv(): jnp.einsum('rco,io->rci', piece, kernel[tap], preferred_element_type=jnp....  13 us
    ppermute x12, waiting for transfers between devices, halve(): lax.ppermute(send, axis, [(i, pos[lab[i] ^ 1 << b]) for i in range(n)])  12.7 us
  transfers between devices with their start and end apart: 28, of which 14 were waited for; matrix products, arithmetic and copies ran while one was open for 31% of the time, Pallas kernels for 0%

profile of v2, /device:TPU:32, one launch (start us, length us, event | category | flops | bytes accessed | tf_op | source)
XLA Modules:
  0.0 280.5 jit_solution(8808427666406043145)
XLA Ops:
  3.0 1.9 collective-permute-start.1
  6.8 6.4 %collective-permute-done = bf16[4,4,384]{2,1,0:T(4,128)(2,1)S(1)} collective-permute-done((bf16[4,4,384]{2,1,0:T(4,128)(2,1)S(1)}, bf16[4,4,384]{2,1,0:T(4,128)(2,1)S(1)}, u32[]{:S(2)}, u32[]{:S(2)}) %collective-permute-start) | collective-permute-done | bytes 12320 | tf_op jit(solution)/shard_map/ppermute | solution.py:9
  14.8 3.2 %collective-permute-start.2 = (bf16[4,136,384]{2,1,0:T(8,128)(2,1)S(1)}, bf16[4,136,384]{2,1,0:T(8,128)(2,1)S(1)}, u32[]{:S(2)}, u32[]{:S(2)}) collective-permute-start(bf16[4,136,384]{2,1,0:T(8,128)(2,1)S(1)} %pad_maximum_fusion.1), channel_id=1, source_target_pairs={{0,16},{16,32},{32,48},{48,64},{64,80},{80,96},{96,112},{112,128},... | collective-permute-start | bytes 1253384 | tf_op jit(solution)/shard_map/ppermute | solution.py:12
  43.3 1.9 convolution_add_fusion.25
  117.5 2.3 constant_dynamic-slice_fusion.11
  121.2 2.0 collective-permute-start.4
  125.3 8.5 %fusion.380 = (f32[12,9,192]{0,2,1:T(8,128)}, f32[12,9,192]{0,2,1:T(8,128)}, f32[12,9,192]{0,2,1:T(8,128)}, f32[12,9,192]{0,2,1:T(8,128)}, f32[12,9,192]{0,2,1:T...) fusion(f32[192,9,192]{0,2,1:T(8,128)S(1)} %fusion.21), kind=kLoop, calls=%fused_computation.548 | loop fusion | bytes 2654208 | tf_op jit(solution)/shard_map/slice | solution.py:84
  133.8 1.9 copy.531
  136.4 1.9 copy.532
  141.8 1.9 copy.535
  147.2 1.9 copy.538
  152.6 1.9 copy.541
  158.0 1.9 copy.544
  171.4 2.9 %fusion.381 = (f32[12,9,192]{2,0,1:T(8,128)S(1)}, f32[12,9,192]{2,0,1:T(8,128)S(1)}, f32[12,9,192]{2,0,1:T(8,128)S(1)}, f32[12,9,192]{2,0,1:T(8,128)S(1)}, f32[1...) fusion(f32[192,9,192]{2,0,1:T(8,128)} %fusion.48), kind=kLoop, calls=%fused_computation.549 | loop fusion | bytes 2654208 | tf_op jit(solution)/shard_map/slice | solution.py:84
  203.5 1.8 fusion.129
  205.4 4.0 %collective-permute-start.5 = (f32[2,2,162,128]{3,2,1,0:T(8,128)S(1)}, f32[2,2,162,128]{3,2,1,0:T(8,128)S(1)}, u32[]{:S(2)}, u32[]{:S(2)}) collective-permute-start(f32[2,2,162,128]{3,2,1,0:T(8,128)S(1)} %bitcast.642), channel_id=1, source_target_pairs={{0,32},{16,48},{32,0},{48,16},{64,96},{80,112},{96,64},{112,80},{1... | collective-permute-start | bytes 995336 | tf_op jit(solution)/shard_map/ppermute | solution.py:92
  211.1 2.1 collective-permute-start.21
  213.2 5.1 %collective-permute-done.5 = f32[2,2,162,128]{3,2,1,0:T(8,128)S(1)} collective-permute-done((f32[2,2,162,128]{3,2,1,0:T(8,128)S(1)}, f32[2,2,162,128]{3,2,1,0:T(8,128)S(1)}, u32[]{:S(2)}, u32[]{:S(2)}) %collective-permute-start.5) | collective-permute-done | bytes 331808 | tf_op jit(solution)/shard_map/ppermute | solution.py:92
  218.4 3.4 %collective-permute-start.6 = (f32[2,162,128]{2,1,0:T(8,128)S(1)}, f32[2,162,128]{2,1,0:T(8,128)S(1)}, u32[]{:S(2)}, u32[]{:S(2)}) collective-permute-start(f32[2,162,128]{2,1,0:T(8,128)S(1)} %dynamic-slice_bitcast_fusion.2), channel_id=1, source_target_pairs={{0,64},{16,80},{32,96},{48,112},{64,0},{80,16},{96,32},{112,48},{1... | collective-permute-start | bytes 497672 | tf_op jit(solution)/shard_map/ppermute | solution.py:92
  221.9 3.9 %collective-permute-done.13 = f32[2,2,162,128]{3,2,1,0:T(8,128)S(1)} collective-permute-done((f32[2,2,162,128]{3,2,1,0:T(8,128)S(1)}, f32[2,2,162,128]{3,2,1,0:T(8,128)S(1)}, u32[]{:S(2)}, u32[]{:S(2)}) %collective-permute-start.13) | collective-permute-done | bytes 331808 | tf_op jit(solution)/shard_map/ppermute | solution.py:92
  225.8 3.6 %collective-permute-start.14 = (f32[2,162,128]{2,1,0:T(8,128)S(1)}, f32[2,162,128]{2,1,0:T(8,128)S(1)}, u32[]{:S(2)}, u32[]{:S(2)}) collective-permute-start(f32[2,162,128]{2,1,0:T(8,128)S(1)} %dynamic-slice_bitcast_fusion.1), channel_id=1, source_target_pairs={{0,64},{16,80},{32,96},{48,112},{64,0},{80,16},{96,32},{112,48},{1... | collective-permute-start | bytes 497672 | tf_op jit(solution)/shard_map/ppermute | solution.py:92
  229.4 3.3 %collective-permute-done.21 = f32[2,2,162,128]{3,2,1,0:T(8,128)S(1)} collective-permute-done((f32[2,2,162,128]{3,2,1,0:T(8,128)S(1)}, f32[2,2,162,128]{3,2,1,0:T(8,128)S(1)}, u32[]{:S(2)}, u32[]{:S(2)}) %collective-permute-start.21) | collective-permute-done | bytes 331808 | tf_op jit(solution)/shard_map/ppermute | solution.py:92
  232.8 3.0 %collective-permute-start.22 = (f32[2,162,128]{2,1,0:T(8,128)S(1)}, f32[2,162,128]{2,1,0:T(8,128)S(1)}, u32[]{:S(2)}, u32[]{:S(2)}) collective-permute-start(f32[2,162,128]{2,1,0:T(8,128)S(1)} %dynamic-slice_bitcast_fusion), channel_id=1, source_target_pairs={{0,64},{16,80},{32,96},{48,112},{64,0},{80,16},{96,32},{112,48},{1... | collective-permute-start | bytes 497672 | tf_op jit(solution)/shard_map/ppermute | solution.py:92
  235.9 2.3 collective-permute-start.7
  239.8 3.6 %collective-permute-start.23 = (f32[162,128]{1,0:T(8,128)S(1)}, f32[162,128]{1,0:T(8,128)S(1)}, u32[]{:S(2)}, u32[]{:S(2)}) collective-permute-start(f32[162,128]{1,0:T(8,128)S(1)} %dynamic-slice_bitcast_fusion.3), channel_id=1, source_target_pairs={{0,192},{16,208},{32,224},{48,240},{64,128},{80,144},{96,160},{112... | collective-permute-start | bytes 248840 | tf_op jit(solution)/shard_map/ppermute | solution.py:92
  243.3 5.7 %collective-permute-start.8 = (f32[162,128]{1,0:T(8,128)S(1)}, f32[162,128]{1,0:T(8,128)S(1)}, u32[]{:S(2)}, u32[]{:S(2)}) collective-permute-start(f32[162,128]{1,0:T(8,128)S(1)} %bitcast_add_fusion.8), channel_id=1, source_target_pairs={{0,1},{1,0},{2,3},{3,2},{4,5},{5,4},{6,7},{7,6},{8,9},{9,8},{10,11... | collective-permute-start | bytes 248840 | tf_op jit(solution)/shard_map/ppermute | solution.py:100
  252.4 1.9 collective-permute-done.16
  254.5 1.9 collective-permute-done.24
  256.8 3.7 %collective-permute-done.9 = f32[162,128]{1,0:T(8,128)S(1)} collective-permute-done((f32[162,128]{1,0:T(8,128)S(1)}, f32[162,128]{1,0:T(8,128)S(1)}, u32[]{:S(2)}, u32[]{:S(2)}) %collective-permute-start.9) | collective-permute-done | bytes 82976 | tf_op jit(solution)/shard_map/ppermute | solution.py:100
  261.9 3.9 %collective-permute-start.18 = (f32[162,128]{1,0:T(8,128)S(1)}, f32[162,128]{1,0:T(8,128)S(1)}, u32[]{:S(2)}, u32[]{:S(2)}) collective-permute-start(f32[162,128]{1,0:T(8,128)S(1)} %add.463), channel_id=1, source_target_pairs={{0,7},{1,6},{2,5},{3,4},{4,3},{5,2},{6,1},{7,0},{8,15},{9,14},{10,... | collective-permute-start | bytes 248840 | tf_op jit(solution)/shard_map/ppermute | solution.py:100
  270.3 2.5 collective-permute-start.19
  277.6 1.8 collective-permute-done.27
  (425 shorter events, 177.5 us)
Async XLA Ops:
  0.6 17.4 %copy-start.57 = (s32[16]{0:T(128)S(1)}, s32[16]{0:T(128)}, u32[]{:S(2)}) copy-start(s32[16]{0:T(128)} %constant.152.clone) | copy-start | bytes 196
  1.7 19.9 %copy-start.2 = (bf16[4,128,192]{2,1,0:T(8,128)(2,1)}, bf16[4,128,192]{2,1,0:T(8,128)(2,1)S(1)}, u32[]{:S(2)}) copy-start(bf16[4,128,192]{2,1,0:T(8,128)(2,1)S(1)} %copy.401) | copy-start | bytes 589828
  2.9 18.8 %copy-start.4 = (bf16[4,128,192]{2,1,0:T(8,128)(2,1)}, bf16[4,128,192]{2,1,0:T(8,128)(2,1)S(1)}, u32[]{:S(2)}) copy-start(bf16[4,128,192]{2,1,0:T(8,128)(2,1)S(1)} %copy.400) | copy-start | bytes 589828
  3.0 3.8 %collective-permute-start.1 = (bf16[4,4,384]{2,1,0:T(4,128)(2,1)S(1)}, bf16[4,4,384]{2,1,0:T(4,128)(2,1)S(1)}, u32[]{:S(2)}, u32[]{:S(2)}) collective-permute-start(bf16[4,4,384]{2,1,0:T(4,128)(2,1)S(1)} %get-tuple-element.81), channel_id=1, source_target_pairs={{0,15},{1,0},{2,1},{3,2},{4,3},{5,4},{6,5},{7,6},{8,7},{9,8},{10,9... | collective-permute-start | bytes 36872 | tf_op jit(solution)/shard_map/ppermute | solution.py:10
  4.9 8.3 %collective-permute-start = (bf16[4,4,384]{2,1,0:T(4,128)(2,1)S(1)}, bf16[4,4,384]{2,1,0:T(4,128)(2,1)S(1)}, u32[]{:S(2)}, u32[]{:S(2)}) collective-permute-start(bf16[4,4,384]{2,1,0:T(4,128)(2,1)S(1)} %get-tuple-element.80), channel_id=1, source_target_pairs={{0,1},{1,2},{2,3},{3,4},{4,5},{5,6},{6,7},{7,8},{8,9},{9,10},{10,1... | collective-permute-start | bytes 36872 | tf_op jit(solution)/shard_map/ppermute | solution.py:9
  13.4 7.9 %collective-permute-start.3 = (bf16[4,136,384]{2,1,0:T(8,128)(2,1)S(1)}, bf16[4,136,384]{2,1,0:T(8,128)(2,1)S(1)}, u32[]{:S(2)}, u32[]{:S(2)}) collective-permute-start(bf16[4,136,384]{2,1,0:T(8,128)(2,1)S(1)} %pad_maximum_fusion.1), channel_id=1, source_target_pairs={{16,0},{32,16},{48,32},{64,48},{80,64},{96,80},{112,96},{128,112},... | collective-permute-start | bytes 1253384 | tf_op jit(solution)/shard_map/ppermute | solution.py:13
  14.8 6.5 %collective-permute-start.2 = (bf16[4,136,384]{2,1,0:T(8,128)(2,1)S(1)}, bf16[4,136,384]{2,1,0:T(8,128)(2,1)S(1)}, u32[]{:S(2)}, u32[]{:S(2)}) collective-permute-start(bf16[4,136,384]{2,1,0:T(8,128)(2,1)S(1)} %pad_maximum_fusion.1), channel_id=1, source_target_pairs={{0,16},{16,32},{32,48},{48,64},{64,80},{80,96},{96,112},{112,128},... | collective-permute-start | bytes 1253384 | tf_op jit(solution)/shard_map/ppermute | solution.py:12
  101.6 15.2 %copy-start.55 = (f32[1,162,128]{2,1,0:T(8,128)S(1)}, f32[1,162,128]{2,1,0:T(8,128)}, u32[]{:S(2)}) copy-start(f32[1,162,128]{2,1,0:T(8,128)} %slice.818) | copy-start | bytes 248836
  121.2 82.2 %collective-permute-start.4 = (f32[2,2,2,162,128]{4,2,3,1,0:T(2,128)}, f32[2,2,2,162,128]{4,2,3,1,0:T(2,128)}, u32[]{:S(2)}, u32[]{:S(2)}) collective-permute-start(f32[2,2,2,162,128]{4,2,3,1,0:T(2,128)} %bitcast.630), channel_id=1, source_target_pairs={{0,16},{16,0},{32,48},{48,32},{64,80},{80,64},{96,112},{112,96},{1... | collective-permute-start | bytes 1990664 | tf_op jit(solution)/shard_map/ppermute | solution.py:92
  201.1 8.3 %collective-permute-start.12 = (f32[2,2,2,162,128]{4,2,3,1,0:T(2,128)S(1)}, f32[2,2,2,162,128]{4,2,3,1,0:T(2,128)S(1)}, u32[]{:S(2)}, u32[]{:S(2)}) collective-permute-start(f32[2,2,2,162,128]{4,2,3,1,0:T(2,128)S(1)} %bitcast.641), channel_id=1, source_target_pairs={{0,16},{16,0},{32,48},{48,32},{64,80},{80,64},{96,112},{112,96},{1... | collective-permute-start | bytes 1990664 | tf_op jit(solution)/shard_map/ppermute | solution.py:92
  203.0 7.4 %collective-permute-start.20 = (f32[2,2,2,162,128]{4,2,3,1,0:T(2,128)S(1)}, f32[2,2,2,162,128]{4,2,3,1,0:T(2,128)S(1)}, u32[]{:S(2)}, u32[]{:S(2)}) collective-permute-start(f32[2,2,2,162,128]{4,2,3,1,0:T(2,128)S(1)} %bitcast.640), channel_id=1, source_target_pairs={{0,16},{16,0},{32,48},{48,32},{64,80},{80,64},{96,112},{112,96},{1... | collective-permute-start | bytes 1990664 | tf_op jit(solution)/shard_map/ppermute | solution.py:92
  205.4 12.9 %collective-permute-start.5 = (f32[2,2,162,128]{3,2,1,0:T(8,128)S(1)}, f32[2,2,162,128]{3,2,1,0:T(8,128)S(1)}, u32[]{:S(2)}, u32[]{:S(2)}) collective-permute-start(f32[2,2,162,128]{3,2,1,0:T(8,128)S(1)} %bitcast.642), channel_id=1, source_target_pairs={{0,32},{16,48},{32,0},{48,16},{64,96},{80,112},{96,64},{112,80},{1... | collective-permute-start | bytes 995336 | tf_op jit(solution)/shard_map/ppermute | solution.py:92
  210.2 15.5 %collective-permute-start.13 = (f32[2,2,162,128]{3,2,1,0:T(8,128)S(1)}, f32[2,2,162,128]{3,2,1,0:T(8,128)S(1)}, u32[]{:S(2)}, u32[]{:S(2)}) collective-permute-start(f32[2,2,162,128]{3,2,1,0:T(8,128)S(1)} %bitcast.643), channel_id=1, source_target_pairs={{0,32},{16,48},{32,0},{48,16},{64,96},{80,112},{96,64},{112,80},{1... | collective-permute-start | bytes 995336 | tf_op jit(solution)/shard_map/ppermute | solution.py:92
  211.1 21.6 %collective-permute-start.21 = (f32[2,2,162,128]{3,2,1,0:T(8,128)S(1)}, f32[2,2,162,128]{3,2,1,0:T(8,128)S(1)}, u32[]{:S(2)}, u32[]{:S(2)}) collective-permute-start(f32[2,2,162,128]{3,2,1,0:T(8,128)S(1)} %bitcast.644), channel_id=1, source_target_pairs={{0,32},{16,48},{32,0},{48,16},{64,96},{80,112},{96,64},{112,80},{1... | collective-permute-start | bytes 995336 | tf_op jit(solution)/shard_map/ppermute | solution.py:92
  218.4 17.4 %collective-permute-start.6 = (f32[2,162,128]{2,1,0:T(8,128)S(1)}, f32[2,162,128]{2,1,0:T(8,128)S(1)}, u32[]{:S(2)}, u32[]{:S(2)}) collective-permute-start(f32[2,162,128]{2,1,0:T(8,128)S(1)} %dynamic-slice_bitcast_fusion.2), channel_id=1, source_target_pairs={{0,64},{16,80},{32,96},{48,112},{64,0},{80,16},{96,32},{112,48},{1... | collective-permute-start | bytes 497672 | tf_op jit(solution)/shard_map/ppermute | solution.py:92
  225.8 12.4 %collective-permute-start.14 = (f32[2,162,128]{2,1,0:T(8,128)S(1)}, f32[2,162,128]{2,1,0:T(8,128)S(1)}, u32[]{:S(2)}, u32[]{:S(2)}) collective-permute-start(f32[2,162,128]{2,1,0:T(8,128)S(1)} %dynamic-slice_bitcast_fusion.1), channel_id=1, source_target_pairs={{0,64},{16,80},{32,96},{48,112},{64,0},{80,16},{96,32},{112,48},{1... | collective-permute-start | bytes 497672 | tf_op jit(solution)/shard_map/ppermute | solution.py:92
  232.8 6.9 %collective-permute-start.22 = (f32[2,162,128]{2,1,0:T(8,128)S(1)}, f32[2,162,128]{2,1,0:T(8,128)S(1)}, u32[]{:S(2)}, u32[]{:S(2)}) collective-permute-start(f32[2,162,128]{2,1,0:T(8,128)S(1)} %dynamic-slice_bitcast_fusion), channel_id=1, source_target_pairs={{0,64},{16,80},{32,96},{48,112},{64,0},{80,16},{96,32},{112,48},{1... | collective-permute-start | bytes 497672 | tf_op jit(solution)/shard_map/ppermute | solution.py:92
  235.9 7.4 %collective-permute-start.7 = (f32[162,128]{1,0:T(8,128)S(1)}, f32[162,128]{1,0:T(8,128)S(1)}, u32[]{:S(2)}, u32[]{:S(2)}) collective-permute-start(f32[162,128]{1,0:T(8,128)S(1)} %dynamic-slice_bitcast_fusion.5), channel_id=1, source_target_pairs={{0,192},{16,208},{32,224},{48,240},{64,128},{80,144},{96,160},{112... | collective-permute-start | bytes 248840 | tf_op jit(solution)/shard_map/ppermute | solution.py:92
  238.2 10.9 %collective-permute-start.15 = (f32[162,128]{1,0:T(8,128)S(1)}, f32[162,128]{1,0:T(8,128)S(1)}, u32[]{:S(2)}, u32[]{:S(2)}) collective-permute-start(f32[162,128]{1,0:T(8,128)S(1)} %dynamic-slice_bitcast_fusion.4), channel_id=1, source_target_pairs={{0,192},{16,208},{32,224},{48,240},{64,128},{80,144},{96,160},{112... | collective-permute-start | bytes 248840 | tf_op jit(solution)/shard_map/ppermute | solution.py:92
  239.8 10.5 %collective-permute-start.23 = (f32[162,128]{1,0:T(8,128)S(1)}, f32[162,128]{1,0:T(8,128)S(1)}, u32[]{:S(2)}, u32[]{:S(2)}) collective-permute-start(f32[162,128]{1,0:T(8,128)S(1)} %dynamic-slice_bitcast_fusion.3), channel_id=1, source_target_pairs={{0,192},{16,208},{32,224},{48,240},{64,128},{80,144},{96,160},{112... | collective-permute-start | bytes 248840 | tf_op jit(solution)/shard_map/ppermute | solution.py:92
  243.3 8.9 %collective-permute-start.8 = (f32[162,128]{1,0:T(8,128)S(1)}, f32[162,128]{1,0:T(8,128)S(1)}, u32[]{:S(2)}, u32[]{:S(2)}) collective-permute-start(f32[162,128]{1,0:T(8,128)S(1)} %bitcast_add_fusion.8), channel_id=1, source_target_pairs={{0,1},{1,0},{2,3},{3,2},{4,5},{5,4},{6,7},{7,6},{8,9},{9,8},{10,11... | collective-permute-start | bytes 248840 | tf_op jit(solution)/shard_map/ppermute | solution.py:100
  249.1 5.2 %collective-permute-start.16 = (f32[162,128]{1,0:T(8,128)S(1)}, f32[162,128]{1,0:T(8,128)S(1)}, u32[]{:S(2)}, u32[]{:S(2)}) collective-permute-start(f32[162,128]{1,0:T(8,128)S(1)} %bitcast_add_fusion.7), channel_id=1, source_target_pairs={{0,1},{1,0},{2,3},{3,2},{4,5},{5,4},{6,7},{7,6},{8,9},{9,8},{10,11... | collective-permute-start | bytes 248840 | tf_op jit(solution)/shard_map/ppermute | solution.py:100
  250.3 6.1 %collective-permute-start.24 = (f32[162,128]{1,0:T(8,128)S(1)}, f32[162,128]{1,0:T(8,128)S(1)}, u32[]{:S(2)}, u32[]{:S(2)}) collective-permute-start(f32[162,128]{1,0:T(8,128)S(1)} %bitcast_add_fusion.6), channel_id=1, source_target_pairs={{0,1},{1,0},{2,3},{3,2},{4,5},{5,4},{6,7},{7,6},{8,9},{9,8},{10,11... | collective-permute-start | bytes 248840 | tf_op jit(solution)/shard_map/ppermute | solution.py:100
  252.3 8.3 %collective-permute-start.9 = (f32[162,128]{1,0:T(8,128)S(1)}, f32[162,128]{1,0:T(8,128)S(1)}, u32[]{:S(2)}, u32[]{:S(2)}) collective-permute-start(f32[162,128]{1,0:T(8,128)S(1)} %add.446), channel_id=1, source_target_pairs={{0,3},{1,2},{2,1},{3,0},{4,7},{5,6},{6,5},{7,4},{8,11},{9,10},{10,... | collective-permute-start | bytes 248840 | tf_op jit(solution)/shard_map/ppermute | solution.py:100
  254.3 7.5 %collective-permute-start.17 = (f32[162,128]{1,0:T(8,128)S(1)}, f32[162,128]{1,0:T(8,128)S(1)}, u32[]{:S(2)}, u32[]{:S(2)}) collective-permute-start(f32[162,128]{1,0:T(8,128)S(1)} %add.462), channel_id=1, source_target_pairs={{0,3},{1,2},{2,1},{3,0},{4,7},{5,6},{6,5},{7,4},{8,11},{9,10},{10,... | collective-permute-start | bytes 248840 | tf_op jit(solution)/shard_map/ppermute | solution.py:100
  256.4 9.4 %collective-permute-start.25 = (f32[162,128]{1,0:T(8,128)S(1)}, f32[162,128]{1,0:T(8,128)S(1)}, u32[]{:S(2)}, u32[]{:S(2)}) collective-permute-start(f32[162,128]{1,0:T(8,128)S(1)} %add.478), channel_id=1, source_target_pairs={{0,3},{1,2},{2,1},{3,0},{4,7},{5,6},{6,5},{7,4},{8,11},{9,10},{10,... | collective-permute-start | bytes 248840 | tf_op jit(solution)/shard_map/ppermute | solution.py:100
  260.5 8.5 %collective-permute-start.10 = (f32[162,128]{1,0:T(8,128)S(1)}, f32[162,128]{1,0:T(8,128)S(1)}, u32[]{:S(2)}, u32[]{:S(2)}) collective-permute-start(f32[162,128]{1,0:T(8,128)S(1)} %add.447), channel_id=1, source_target_pairs={{0,7},{1,6},{2,5},{3,4},{4,3},{5,2},{6,1},{7,0},{8,15},{9,14},{10,... | collective-permute-start | bytes 248840 | tf_op jit(solution)/shard_map/ppermute | solution.py:100
  261.9 8.4 %collective-permute-start.18 = (f32[162,128]{1,0:T(8,128)S(1)}, f32[162,128]{1,0:T(8,128)S(1)}, u32[]{:S(2)}, u32[]{:S(2)}) collective-permute-start(f32[162,128]{1,0:T(8,128)S(1)} %add.463), channel_id=1, source_target_pairs={{0,7},{1,6},{2,5},{3,4},{4,3},{5,2},{6,1},{7,0},{8,15},{9,14},{10,... | collective-permute-start | bytes 248840 | tf_op jit(solution)/shard_map/ppermute | solution.py:100
  265.8 7.6 %collective-permute-start.26 = (f32[162,128]{1,0:T(8,128)S(1)}, f32[162,128]{1,0:T(8,128)S(1)}, u32[]{:S(2)}, u32[]{:S(2)}) collective-permute-start(f32[162,128]{1,0:T(8,128)S(1)} %add.479), channel_id=1, source_target_pairs={{0,7},{1,6},{2,5},{3,4},{4,3},{5,2},{6,1},{7,0},{8,15},{9,14},{10,... | collective-permute-start | bytes 248840 | tf_op jit(solution)/shard_map/ppermute | solution.py:100
  269.0 6.9 %collective-permute-start.11 = (f32[162,128]{1,0:T(8,128)S(1)}, f32[162,128]{1,0:T(8,128)S(1)}, u32[]{:S(2)}, u32[]{:S(2)}) collective-permute-start(f32[162,128]{1,0:T(8,128)S(1)} %add.448), channel_id=1, source_target_pairs={{0,8},{1,9},{2,10},{3,11},{4,12},{5,13},{6,14},{7,15},{8,0},{9,1},... | collective-permute-start | bytes 248840 | tf_op jit(solution)/shard_map/ppermute | solution.py:100
  270.3 6.5 %collective-permute-start.19 = (f32[162,128]{1,0:T(8,128)S(1)}, f32[162,128]{1,0:T(8,128)S(1)}, u32[]{:S(2)}, u32[]{:S(2)}) collective-permute-start(f32[162,128]{1,0:T(8,128)S(1)} %add.464), channel_id=1, source_target_pairs={{0,8},{1,9},{2,10},{3,11},{4,12},{5,13},{6,14},{7,15},{8,0},{9,1},... | collective-permute-start | bytes 248840 | tf_op jit(solution)/shard_map/ppermute | solution.py:100
  273.4 6.1 %collective-permute-start.27 = (f32[162,128]{1,0:T(8,128)S(1)}, f32[162,128]{1,0:T(8,128)S(1)}, u32[]{:S(2)}, u32[]{:S(2)}) collective-permute-start(f32[162,128]{1,0:T(8,128)S(1)} %add.480), channel_id=1, source_target_pairs={{0,8},{1,9},{2,10},{3,11},{4,12},{5,13},{6,14},{7,15},{8,0},{9,1},... | collective-permute-start | bytes 248840 | tf_op jit(solution)/shard_map/ppermute | solution.py:100
  (54 other events, 285.6 us)

commit v3 on v2

--- a/solution.py
+++ b/solution.py
@@ -81,7 +81,12 @@
     n = lax.axis_size(axis)
     bits = n.bit_length() - 1
     lab, pos = labels(axis)
-    x = jnp.stack([x[pos[l]] for l in range(n)])
+    runs, first = [], 0
+    for l in range(1, n + 1):
+        if l == n or pos[l] != pos[l - 1] + 1:
+            runs.append(x[pos[first] : pos[l - 1] + 1])
+            first = l
+    x = jnp.concatenate(runs) if len(runs) > 1 else x
     me = jnp.asarray(lab, jnp.int32)[lax.axis_index(axis)]
     x = x.reshape((2,) * bits + x.shape[1:])
     x = x.transpose(tuple(range(bits - 1, -1, -1)) + tuple(range(bits, x.ndim)))

time: 285 us -> 171 us (0.60)
  local copies, waits for them, and re-layouts: 149 us -> 43.7 us
  waiting for transfers between devices: 34 us -> 26.2 us
  matrix products: 36.9 us -> 29.6 us
  starting transfers between devices: 51.4 us -> 55.9 us
  other arithmetic: 4.39 us -> 8.08 us
    slice x99 -> x24, local copies, waits for them, and re-layouts: 107 us -> 30.5 us  [halve(): runs.append(x[pos[first]:pos[l - 1] + 1])]
    unnamed x169 -> x54, local copies, waits for them, and re-layouts: 37.4 us -> 10.5 us
    ppermute x12, starting transfers between devices: 19.2 us -> 28.1 us  [all_sum(): x = x + lax.ppermute(x, axis, [(i, pos[lab[i] ^ 1 << b]) for i in range(n)])]
    ppermute x12, waiting for transfers between devices: 13.3 us -> 5.71 us  [all_sum(): x = x + lax.ppermute(x, axis, [(i, pos[lab[i] ^ 1 << b]) for i in range(n)])]
    dot_general x27, matrix products: 14.4 us -> 8.54 us  [kernel_grad(): jnp.einsum('rci,rco->oi', piece, delta, preferred_element_type=jnp.float32)]
    ppermute x1, waiting for transfers between devices: 6.4 us -> 1.67 us  [exchange(): lax.ppermute(x[:, -h:], 'lon', [(j, (j + 1) % nlon) for j in range(nlon)])]
    ppermute x12, waiting for transfers between devices: 12.7 us -> 16.3 us  [halve(): lax.ppermute(send, axis, [(i, pos[lab[i] ^ 1 << b]) for i in range(n)])]
  transfers between devices with their start and end apart: 28 -> 28, of which waited for: 14 -> 11; matrix products, arithmetic and copies ran while one was open for 31% -> 13% of each run, Pallas kernels for 0% -> 0%
where the time goes in v3:
time: 171 us; the launch traced here: 168 us
  starting transfers between devices  55.9 us (33%)
  local copies, waits for them, and re-layouts  43.7 us (26%)
  matrix products  29.6 us (17%)
  waiting for transfers between devices  26.2 us (15%)
  other arithmetic  8.08 us (5%)
  between operations  4.41 us (3%)
    slice x24, local copies, waits for them, and re-layouts, halve(): runs.append(x[pos[first]:pos[l - 1] + 1])  30.5 us
    ppermute x12, starting transfers between devices, all_sum(): x = x + lax.ppermute(x, axis, [(i, pos[lab[i] ^ 1 << b]) for i in range(n)])  28.1 us
    ppermute x12, starting transfers between devices, halve(): lax.ppermute(send, axis, [(i, pos[lab[i] ^ 1 << b]) for i in range(n)])  22.8 us
    ppermute x12, waiting for transfers between devices, halve(): lax.ppermute(send, axis, [(i, pos[lab[i] ^ 1 << b]) for i in range(n)])  16.3 us
    dot_general x27, matrix products, adjoint_conv(): jnp.einsum('rco,io->rci', piece, kernel[tap], preferred_element_type=jnp....  10.8 us
    unnamed x54, local copies, waits for them, and re-layouts  10.5 us
    dot_general x27, matrix products, forward_conv(): jnp.einsum('rci,io->rco', piece, kernel[tap], preferred_element_type=jnp....  10.3 us
    dot_general x27, matrix products, kernel_grad(): jnp.einsum('rci,rco->oi', piece, delta, preferred_element_type=jnp.float32)  8.54 us
  transfers between devices with their start and end apart: 28, of which 11 were waited for; matrix products, arithmetic and copies ran while one was open for 13% of the time, Pallas kernels for 0%

profile of v3, /device:TPU:32, one launch (start us, length us, event | category | flops | bytes accessed | tf_op | source)
XLA Modules:
  0.0 167.9 jit_solution(15977881333096747957)
XLA Ops:
  2.9 2.0 %collective-permute-start = (bf16[4,4,384]{2,1,0:T(4,128)(2,1)S(1)}, bf16[4,4,384]{2,1,0:T(4,128)(2,1)S(1)}, u32[]{:S(2)}, u32[]{:S(2)}) collective-permute-start(bf16[4,4,384]{2,1,0:T(4,128)(2,1)S(1)} %get-tuple-element.38), channel_id=1, source_target_pairs={{0,1},{1,2},{2,3},{3,4},{4,5},{5,6},{6,7},{7,8},{8,9},{9,10},{10,1... | collective-permute-start | bytes 36872 | tf_op jit(solution)/shard_map/ppermute | solution.py:9
  5.0 1.7 collective-permute-done
  6.6 1.9 %collective-permute-done.1 = bf16[4,4,384]{2,1,0:T(4,128)(2,1)S(1)} collective-permute-done((bf16[4,4,384]{2,1,0:T(4,128)(2,1)S(1)}, bf16[4,4,384]{2,1,0:T(4,128)(2,1)S(1)}, u32[]{:S(2)}, u32[]{:S(2)}) %collective-permute-start.1) | collective-permute-done | bytes 12320 | tf_op jit(solution)/shard_map/ppermute | solution.py:10
  35.7 1.7 %fusion.380 = (f32[48,9,192]{0,2,1:T(8,128)}, f32[48,9,192]{0,2,1:T(8,128)}) fusion(f32[192,9,192]{0,2,1:T(8,128)S(1)} %fusion.21), kind=kLoop, calls=%fused_computation.503 | loop fusion | bytes 1327104 | tf_op jit(solution)/shard_map/slice | solution.py:87
  54.0 2.4 %copy.427 = f32[96,9,192]{2,1,0:T(8,128)S(1)} copy(f32[96,9,192]{0,2,1:T(8,128)} %slice.653) | data formatting | bytes 1327104 | tf_op jit(solution)/shard_map/slice | solution.py:87
  57.9 2.9 %copy.428 = f32[48,9,192]{2,1,0:T(8,128)} copy(f32[48,9,192]{0,2,1:T(8,128)} %get-tuple-element.20) | data formatting | bytes 663552 | tf_op jit(solution)/shard_map/slice | solution.py:87
  60.7 2.1 %slice.578 = f32[4,162,128]{2,1,0:T(8,128)} reshape(f32[48,9,192]{2,1,0:T(8,128)} %copy.428) | data formatting | bytes 663552 | tf_op jit(solution)/shard_map/slice | solution.py:87
  62.9 1.8 %copy.429 = f32[48,9,192]{2,1,0:T(8,128)} copy(f32[48,9,192]{0,2,1:T(8,128)S(1)} %copy-done.3) | data formatting | bytes 663552 | tf_op jit(solution)/shard_map/slice | solution.py:87
  64.7 2.1 %slice.580 = f32[4,162,128]{2,1,0:T(8,128)} reshape(f32[48,9,192]{2,1,0:T(8,128)} %copy.429) | data formatting | bytes 663552 | tf_op jit(solution)/shard_map/slice | solution.py:87
  71.1 8.0 %collective-permute-start.20 = (f32[2,2,2,162,128]{4,2,3,1,0:T(2,128)}, f32[2,2,2,162,128]{4,2,3,1,0:T(2,128)}, u32[]{:S(2)}, u32[]{:S(2)}) collective-permute-start(f32[2,2,2,162,128]{4,2,3,1,0:T(2,128)} %bitcast.628), channel_id=1, source_target_pairs={{0,16},{16,0},{32,48},{48,32},{64,80},{80,64},{96,112},{112,96},{1... | collective-permute-start | bytes 1990664 | tf_op jit(solution)/shard_map/ppermute | solution.py:97
  93.8 1.8 %fusion.127 = f32[2,2,2,162,128]{4,2,3,1,0:T(2,128)S(1)} fusion(f32[2,2,2,162,128]{4,2,3,1,0:T(2,128)} %collective-permute-done.20, f32[2,2,2,1,162,128]{5,4,3,2,1,0:T(8,128)S(1)} %copy-done.7), kind=kLoop, calls=%fused_computation.198 | loop fusion | flops 165888 | bytes 1990656 | tf_op jit(solution)/shard_map/add | solution.py:97
  95.7 1.6 collective-permute-start.21
  97.3 1.8 %fusion.128 = f32[2,2,2,162,128]{4,2,3,1,0:T(2,128)S(1)} fusion(f32[2,2,2,162,128]{4,2,3,1,0:T(2,128)} %collective-permute-done.12, f32[2,2,2,1,162,128]{5,4,3,2,1,0:T(8,128)S(1)} %copy-done.6), kind=kLoop, calls=%fused_computation.201 | loop fusion | flops 165888 | bytes 1990656 | tf_op jit(solution)/shard_map/add | solution.py:97
  102.4 4.3 %collective-permute-done.21 = f32[2,2,162,128]{3,2,1,0:T(8,128)S(1)} collective-permute-done((f32[2,2,162,128]{3,2,1,0:T(8,128)S(1)}, f32[2,2,162,128]{3,2,1,0:T(8,128)S(1)}, u32[]{:S(2)}, u32[]{:S(2)}) %collective-permute-start.21) | collective-permute-done | bytes 331808 | tf_op jit(solution)/shard_map/ppermute | solution.py:97
  106.8 1.7 collective-permute-start.22
  108.5 5.6 %collective-permute-done.13 = f32[2,2,162,128]{3,2,1,0:T(8,128)S(1)} collective-permute-done((f32[2,2,162,128]{3,2,1,0:T(8,128)S(1)}, f32[2,2,162,128]{3,2,1,0:T(8,128)S(1)}, u32[]{:S(2)}, u32[]{:S(2)}) %collective-permute-start.13) | collective-permute-done | bytes 331808 | tf_op jit(solution)/shard_map/ppermute | solution.py:97
  114.2 1.7 collective-permute-start.14
  115.9 4.9 %collective-permute-done.5 = f32[2,2,162,128]{3,2,1,0:T(8,128)S(1)} collective-permute-done((f32[2,2,162,128]{3,2,1,0:T(8,128)S(1)}, f32[2,2,162,128]{3,2,1,0:T(8,128)S(1)}, u32[]{:S(2)}, u32[]{:S(2)}) %collective-permute-start.5) | collective-permute-done | bytes 331808 | tf_op jit(solution)/shard_map/ppermute | solution.py:97
  120.9 1.7 collective-permute-start.6
  122.6 2.0 %collective-permute-start.23 = (f32[162,128]{1,0:T(8,128)S(1)}, f32[162,128]{1,0:T(8,128)S(1)}, u32[]{:S(2)}, u32[]{:S(2)}) collective-permute-start(f32[162,128]{1,0:T(8,128)S(1)} %dynamic-slice_bitcast_fusion.3), channel_id=1, source_target_pairs={{0,192},{16,208},{32,224},{48,240},{64,128},{80,144},{96,160},{112... | collective-permute-start | bytes 248840 | tf_op jit(solution)/shard_map/ppermute | solution.py:97
  126.7 1.8 %collective-permute-start.7 = (f32[162,128]{1,0:T(8,128)S(1)}, f32[162,128]{1,0:T(8,128)S(1)}, u32[]{:S(2)}, u32[]{:S(2)}) collective-permute-start(f32[162,128]{1,0:T(8,128)S(1)} %dynamic-slice_bitcast_fusion.5), channel_id=1, source_target_pairs={{0,192},{16,208},{32,224},{48,240},{64,128},{80,144},{96,160},{112... | collective-permute-start | bytes 248840 | tf_op jit(solution)/shard_map/ppermute | solution.py:97
  129.3 4.6 %collective-permute-start.24 = (f32[162,128]{1,0:T(8,128)S(1)}, f32[162,128]{1,0:T(8,128)S(1)}, u32[]{:S(2)}, u32[]{:S(2)}) collective-permute-start(f32[162,128]{1,0:T(8,128)S(1)} %bitcast_add_fusion.6), channel_id=1, source_target_pairs={{0,1},{1,0},{2,3},{3,2},{4,5},{5,4},{6,7},{7,6},{8,9},{9,8},{10,11... | collective-permute-start | bytes 248840 | tf_op jit(solution)/shard_map/ppermute | solution.py:105
  133.9 1.8 %collective-permute-start.16 = (f32[162,128]{1,0:T(8,128)S(1)}, f32[162,128]{1,0:T(8,128)S(1)}, u32[]{:S(2)}, u32[]{:S(2)}) collective-permute-start(f32[162,128]{1,0:T(8,128)S(1)} %bitcast_add_fusion.7), channel_id=1, source_target_pairs={{0,1},{1,0},{2,3},{3,2},{4,5},{5,4},{6,7},{7,6},{8,9},{9,8},{10,11... | collective-permute-start | bytes 248840 | tf_op jit(solution)/shard_map/ppermute | solution.py:105
  137.4 1.9 %collective-permute-start.25 = (f32[162,128]{1,0:T(8,128)S(1)}, f32[162,128]{1,0:T(8,128)S(1)}, u32[]{:S(2)}, u32[]{:S(2)}) collective-permute-start(f32[162,128]{1,0:T(8,128)S(1)} %add.478), channel_id=1, source_target_pairs={{0,3},{1,2},{2,1},{3,0},{4,7},{5,6},{6,5},{7,4},{8,11},{9,10},{10,... | collective-permute-start | bytes 248840 | tf_op jit(solution)/shard_map/ppermute | solution.py:105
  139.3 1.9 %collective-permute-start.17 = (f32[162,128]{1,0:T(8,128)S(1)}, f32[162,128]{1,0:T(8,128)S(1)}, u32[]{:S(2)}, u32[]{:S(2)}) collective-permute-start(f32[162,128]{1,0:T(8,128)S(1)} %add.462), channel_id=1, source_target_pairs={{0,3},{1,2},{2,1},{3,0},{4,7},{5,6},{6,5},{7,4},{8,11},{9,10},{10,... | collective-permute-start | bytes 248840 | tf_op jit(solution)/shard_map/ppermute | solution.py:105
  142.6 4.0 %collective-permute-done.25 = f32[162,128]{1,0:T(8,128)S(1)} collective-permute-done((f32[162,128]{1,0:T(8,128)S(1)}, f32[162,128]{1,0:T(8,128)S(1)}, u32[]{:S(2)}, u32[]{:S(2)}) %collective-permute-start.25) | collective-permute-done | bytes 82976 | tf_op jit(solution)/shard_map/ppermute | solution.py:105
  146.6 3.4 %collective-permute-start.26 = (f32[162,128]{1,0:T(8,128)S(1)}, f32[162,128]{1,0:T(8,128)S(1)}, u32[]{:S(2)}, u32[]{:S(2)}) collective-permute-start(f32[162,128]{1,0:T(8,128)S(1)} %add.479), channel_id=1, source_target_pairs={{0,7},{1,6},{2,5},{3,4},{4,3},{5,2},{6,1},{7,0},{8,15},{9,14},{10,... | collective-permute-start | bytes 248840 | tf_op jit(solution)/shard_map/ppermute | solution.py:105
  150.0 1.8 %collective-permute-start.18 = (f32[162,128]{1,0:T(8,128)S(1)}, f32[162,128]{1,0:T(8,128)S(1)}, u32[]{:S(2)}, u32[]{:S(2)}) collective-permute-start(f32[162,128]{1,0:T(8,128)S(1)} %add.463), channel_id=1, source_target_pairs={{0,7},{1,6},{2,5},{3,4},{4,3},{5,2},{6,1},{7,0},{8,15},{9,14},{10,... | collective-permute-start | bytes 248840 | tf_op jit(solution)/shard_map/ppermute | solution.py:105
  151.8 3.4 %collective-permute-start.10 = (f32[162,128]{1,0:T(8,128)S(1)}, f32[162,128]{1,0:T(8,128)S(1)}, u32[]{:S(2)}, u32[]{:S(2)}) collective-permute-start(f32[162,128]{1,0:T(8,128)S(1)} %add.447), channel_id=1, source_target_pairs={{0,7},{1,6},{2,5},{3,4},{4,3},{5,2},{6,1},{7,0},{8,15},{9,14},{10,... | collective-permute-start | bytes 248840 | tf_op jit(solution)/shard_map/ppermute | solution.py:105
  155.5 3.1 %collective-permute-start.27 = (f32[162,128]{1,0:T(8,128)S(1)}, f32[162,128]{1,0:T(8,128)S(1)}, u32[]{:S(2)}, u32[]{:S(2)}) collective-permute-start(f32[162,128]{1,0:T(8,128)S(1)} %add.480), channel_id=1, source_target_pairs={{0,8},{1,9},{2,10},{3,11},{4,12},{5,13},{6,14},{7,15},{8,0},{9,1},... | collective-permute-start | bytes 248840 | tf_op jit(solution)/shard_map/ppermute | solution.py:105
  158.6 2.1 %collective-permute-start.19 = (f32[162,128]{1,0:T(8,128)S(1)}, f32[162,128]{1,0:T(8,128)S(1)}, u32[]{:S(2)}, u32[]{:S(2)}) collective-permute-start(f32[162,128]{1,0:T(8,128)S(1)} %add.464), channel_id=1, source_target_pairs={{0,8},{1,9},{2,10},{3,11},{4,12},{5,13},{6,14},{7,15},{8,0},{9,1},... | collective-permute-start | bytes 248840 | tf_op jit(solution)/shard_map/ppermute | solution.py:105
  160.7 1.7 %collective-permute-start.11 = (f32[162,128]{1,0:T(8,128)S(1)}, f32[162,128]{1,0:T(8,128)S(1)}, u32[]{:S(2)}, u32[]{:S(2)}) collective-permute-start(f32[162,128]{1,0:T(8,128)S(1)} %add.448), channel_id=1, source_target_pairs={{0,8},{1,9},{2,10},{3,11},{4,12},{5,13},{6,14},{7,15},{8,0},{9,1},... | collective-permute-start | bytes 248840 | tf_op jit(solution)/shard_map/ppermute | solution.py:105
  (235 shorter events, 78.5 us)
Async XLA Ops:
  0.6 11.1 %copy-start.22 = (s32[16]{0:T(128)S(1)}, s32[16]{0:T(128)}, u32[]{:S(2)}) copy-start(s32[16]{0:T(128)} %constant.152.clone) | copy-start | bytes 196
  2.9 3.8 %collective-permute-start = (bf16[4,4,384]{2,1,0:T(4,128)(2,1)S(1)}, bf16[4,4,384]{2,1,0:T(4,128)(2,1)S(1)}, u32[]{:S(2)}, u32[]{:S(2)}) collective-permute-start(bf16[4,4,384]{2,1,0:T(4,128)(2,1)S(1)} %get-tuple-element.38), channel_id=1, source_target_pairs={{0,1},{1,2},{2,3},{3,4},{4,5},{5,6},{6,7},{7,8},{8,9},{9,10},{10,1... | collective-permute-start | bytes 36872 | tf_op jit(solution)/shard_map/ppermute | solution.py:9
  4.9 3.7 %collective-permute-start.1 = (bf16[4,4,384]{2,1,0:T(4,128)(2,1)S(1)}, bf16[4,4,384]{2,1,0:T(4,128)(2,1)S(1)}, u32[]{:S(2)}, u32[]{:S(2)}) collective-permute-start(bf16[4,4,384]{2,1,0:T(4,128)(2,1)S(1)} %get-tuple-element.39), channel_id=1, source_target_pairs={{0,15},{1,0},{2,1},{3,2},{4,3},{5,4},{6,5},{7,6},{8,7},{9,8},{10,9... | collective-permute-start | bytes 36872 | tf_op jit(solution)/shard_map/ppermute | solution.py:10
  8.8 7.1 %copy-start = (bf16[9,192,192]{2,1,0:T(8,128)(2,1)S(1)}, bf16[9,192,192]{2,1,0:T(8,128)(2,1)}, u32[]{:S(2)}) copy-start(bf16[9,192,192]{2,1,0:T(8,128)(2,1)} %param.9) | copy-start | bytes 1990660
  8.8 6.2 %collective-permute-start.2 = (bf16[4,136,384]{2,1,0:T(8,128)(2,1)S(1)}, bf16[4,136,384]{2,1,0:T(8,128)(2,1)S(1)}, u32[]{:S(2)}, u32[]{:S(2)}) collective-permute-start(bf16[4,136,384]{2,1,0:T(8,128)(2,1)S(1)} %pad_maximum_fusion.4), channel_id=1, source_target_pairs={{0,16},{16,32},{32,48},{48,64},{64,80},{80,96},{96,112},{112,128},... | collective-permute-start | bytes 1253384 | tf_op jit(solution)/shard_map/ppermute | solution.py:12
  10.3 5.4 %collective-permute-start.3 = (bf16[4,136,384]{2,1,0:T(8,128)(2,1)S(1)}, bf16[4,136,384]{2,1,0:T(8,128)(2,1)S(1)}, u32[]{:S(2)}, u32[]{:S(2)}) collective-permute-start(bf16[4,136,384]{2,1,0:T(8,128)(2,1)S(1)} %pad_maximum_fusion.4), channel_id=1, source_target_pairs={{16,0},{32,16},{48,32},{64,48},{80,64},{96,80},{112,96},{128,112},... | collective-permute-start | bytes 1253384 | tf_op jit(solution)/shard_map/ppermute | solution.py:13
  57.9 5.0 %copy-start.3 = (f32[48,9,192]{0,2,1:T(8,128)S(1)}, f32[48,9,192]{0,2,1:T(8,128)}, u32[]{:S(2)}) copy-start(f32[48,9,192]{0,2,1:T(8,128)} %get-tuple-element.21) | copy-start | bytes 995332
  69.7 10.7 %copy-start.4 = (f32[96,9,192]{2,0,1:T(8,128)S(1)}, f32[96,9,192]{2,0,1:T(8,128)}, u32[]{:S(2)}) copy-start(f32[96,9,192]{2,0,1:T(8,128)} %slice.637) | copy-start | bytes 1990660
  71.1 22.2 %collective-permute-start.20 = (f32[2,2,2,162,128]{4,2,3,1,0:T(2,128)}, f32[2,2,2,162,128]{4,2,3,1,0:T(2,128)}, u32[]{:S(2)}, u32[]{:S(2)}) collective-permute-start(f32[2,2,2,162,128]{4,2,3,1,0:T(2,128)} %bitcast.628), channel_id=1, source_target_pairs={{0,16},{16,0},{32,48},{48,32},{64,80},{80,64},{96,112},{112,96},{1... | collective-permute-start | bytes 1990664 | tf_op jit(solution)/shard_map/ppermute | solution.py:97
  80.4 16.9 %collective-permute-start.12 = (f32[2,2,2,162,128]{4,2,3,1,0:T(2,128)}, f32[2,2,2,162,128]{4,2,3,1,0:T(2,128)}, u32[]{:S(2)}, u32[]{:S(2)}) collective-permute-start(f32[2,2,2,162,128]{4,2,3,1,0:T(2,128)} %bitcast.629), channel_id=1, source_target_pairs={{0,16},{16,0},{32,48},{48,32},{64,80},{80,64},{96,112},{112,96},{1... | collective-permute-start | bytes 1990664 | tf_op jit(solution)/shard_map/ppermute | solution.py:97
  88.8 11.4 %collective-permute-start.4 = (f32[2,2,2,162,128]{4,2,3,1,0:T(2,128)S(1)}, f32[2,2,2,162,128]{4,2,3,1,0:T(2,128)S(1)}, u32[]{:S(2)}, u32[]{:S(2)}) collective-permute-start(f32[2,2,2,162,128]{4,2,3,1,0:T(2,128)S(1)} %bitcast.640), channel_id=1, source_target_pairs={{0,16},{16,0},{32,48},{48,32},{64,80},{80,64},{96,112},{112,96},{1... | collective-permute-start | bytes 1990664 | tf_op jit(solution)/shard_map/ppermute | solution.py:97
  95.7 11.0 %collective-permute-start.21 = (f32[2,2,162,128]{3,2,1,0:T(8,128)S(1)}, f32[2,2,162,128]{3,2,1,0:T(8,128)S(1)}, u32[]{:S(2)}, u32[]{:S(2)}) collective-permute-start(f32[2,2,162,128]{3,2,1,0:T(8,128)S(1)} %bitcast.641), channel_id=1, source_target_pairs={{0,32},{16,48},{32,0},{48,16},{64,96},{80,112},{96,64},{112,80},{1... | collective-permute-start | bytes 995336 | tf_op jit(solution)/shard_map/ppermute | solution.py:97
  99.2 14.9 %collective-permute-start.13 = (f32[2,2,162,128]{3,2,1,0:T(8,128)S(1)}, f32[2,2,162,128]{3,2,1,0:T(8,128)S(1)}, u32[]{:S(2)}, u32[]{:S(2)}) collective-permute-start(f32[2,2,162,128]{3,2,1,0:T(8,128)S(1)} %bitcast.642), channel_id=1, source_target_pairs={{0,32},{16,48},{32,0},{48,16},{64,96},{80,112},{96,64},{112,80},{1... | collective-permute-start | bytes 995336 | tf_op jit(solution)/shard_map/ppermute | solution.py:97
  101.0 19.8 %collective-permute-start.5 = (f32[2,2,162,128]{3,2,1,0:T(8,128)S(1)}, f32[2,2,162,128]{3,2,1,0:T(8,128)S(1)}, u32[]{:S(2)}, u32[]{:S(2)}) collective-permute-start(f32[2,2,162,128]{3,2,1,0:T(8,128)S(1)} %bitcast.643), channel_id=1, source_target_pairs={{0,32},{16,48},{32,0},{48,16},{64,96},{80,112},{96,64},{112,80},{1... | collective-permute-start | bytes 995336 | tf_op jit(solution)/shard_map/ppermute | solution.py:97
  106.8 15.7 %collective-permute-start.22 = (f32[2,162,128]{2,1,0:T(8,128)S(1)}, f32[2,162,128]{2,1,0:T(8,128)S(1)}, u32[]{:S(2)}, u32[]{:S(2)}) collective-permute-start(f32[2,162,128]{2,1,0:T(8,128)S(1)} %dynamic-slice_bitcast_fusion), channel_id=1, source_target_pairs={{0,64},{16,80},{32,96},{48,112},{64,0},{80,16},{96,32},{112,48},{1... | collective-permute-start | bytes 497672 | tf_op jit(solution)/shard_map/ppermute | solution.py:97
  114.2 10.4 %collective-permute-start.14 = (f32[2,162,128]{2,1,0:T(8,128)S(1)}, f32[2,162,128]{2,1,0:T(8,128)S(1)}, u32[]{:S(2)}, u32[]{:S(2)}) collective-permute-start(f32[2,162,128]{2,1,0:T(8,128)S(1)} %dynamic-slice_bitcast_fusion.1), channel_id=1, source_target_pairs={{0,64},{16,80},{32,96},{48,112},{64,0},{80,16},{96,32},{112,48},{1... | collective-permute-start | bytes 497672 | tf_op jit(solution)/shard_map/ppermute | solution.py:97
  120.9 5.8 %collective-permute-start.6 = (f32[2,162,128]{2,1,0:T(8,128)S(1)}, f32[2,162,128]{2,1,0:T(8,128)S(1)}, u32[]{:S(2)}, u32[]{:S(2)}) collective-permute-start(f32[2,162,128]{2,1,0:T(8,128)S(1)} %dynamic-slice_bitcast_fusion.2), channel_id=1, source_target_pairs={{0,64},{16,80},{32,96},{48,112},{64,0},{80,16},{96,32},{112,48},{1... | collective-permute-start | bytes 497672 | tf_op jit(solution)/shard_map/ppermute | solution.py:97
  122.6 6.7 %collective-permute-start.23 = (f32[162,128]{1,0:T(8,128)S(1)}, f32[162,128]{1,0:T(8,128)S(1)}, u32[]{:S(2)}, u32[]{:S(2)}) collective-permute-start(f32[162,128]{1,0:T(8,128)S(1)} %dynamic-slice_bitcast_fusion.3), channel_id=1, source_target_pairs={{0,192},{16,208},{32,224},{48,240},{64,128},{80,144},{96,160},{112... | collective-permute-start | bytes 248840 | tf_op jit(solution)/shard_map/ppermute | solution.py:97
  124.6 9.2 %collective-permute-start.15 = (f32[162,128]{1,0:T(8,128)S(1)}, f32[162,128]{1,0:T(8,128)S(1)}, u32[]{:S(2)}, u32[]{:S(2)}) collective-permute-start(f32[162,128]{1,0:T(8,128)S(1)} %dynamic-slice_bitcast_fusion.4), channel_id=1, source_target_pairs={{0,192},{16,208},{32,224},{48,240},{64,128},{80,144},{96,160},{112... | collective-permute-start | bytes 248840 | tf_op jit(solution)/shard_map/ppermute | solution.py:97
  126.7 8.9 %collective-permute-start.7 = (f32[162,128]{1,0:T(8,128)S(1)}, f32[162,128]{1,0:T(8,128)S(1)}, u32[]{:S(2)}, u32[]{:S(2)}) collective-permute-start(f32[162,128]{1,0:T(8,128)S(1)} %dynamic-slice_bitcast_fusion.5), channel_id=1, source_target_pairs={{0,192},{16,208},{32,224},{48,240},{64,128},{80,144},{96,160},{112... | collective-permute-start | bytes 248840 | tf_op jit(solution)/shard_map/ppermute | solution.py:97
  129.3 8.1 %collective-permute-start.24 = (f32[162,128]{1,0:T(8,128)S(1)}, f32[162,128]{1,0:T(8,128)S(1)}, u32[]{:S(2)}, u32[]{:S(2)}) collective-permute-start(f32[162,128]{1,0:T(8,128)S(1)} %bitcast_add_fusion.6), channel_id=1, source_target_pairs={{0,1},{1,0},{2,3},{3,2},{4,5},{5,4},{6,7},{7,6},{8,9},{9,8},{10,11... | collective-permute-start | bytes 248840 | tf_op jit(solution)/shard_map/ppermute | solution.py:105
  133.9 5.4 %collective-permute-start.16 = (f32[162,128]{1,0:T(8,128)S(1)}, f32[162,128]{1,0:T(8,128)S(1)}, u32[]{:S(2)}, u32[]{:S(2)}) collective-permute-start(f32[162,128]{1,0:T(8,128)S(1)} %bitcast_add_fusion.7), channel_id=1, source_target_pairs={{0,1},{1,0},{2,3},{3,2},{4,5},{5,4},{6,7},{7,6},{8,9},{9,8},{10,11... | collective-permute-start | bytes 248840 | tf_op jit(solution)/shard_map/ppermute | solution.py:105
  135.7 5.5 %collective-permute-start.8 = (f32[162,128]{1,0:T(8,128)S(1)}, f32[162,128]{1,0:T(8,128)S(1)}, u32[]{:S(2)}, u32[]{:S(2)}) collective-permute-start(f32[162,128]{1,0:T(8,128)S(1)} %bitcast_add_fusion.8), channel_id=1, source_target_pairs={{0,1},{1,0},{2,3},{3,2},{4,5},{5,4},{6,7},{7,6},{8,9},{9,8},{10,11... | collective-permute-start | bytes 248840 | tf_op jit(solution)/shard_map/ppermute | solution.py:105
  137.4 9.2 %collective-permute-start.25 = (f32[162,128]{1,0:T(8,128)S(1)}, f32[162,128]{1,0:T(8,128)S(1)}, u32[]{:S(2)}, u32[]{:S(2)}) collective-permute-start(f32[162,128]{1,0:T(8,128)S(1)} %add.478), channel_id=1, source_target_pairs={{0,3},{1,2},{2,1},{3,0},{4,7},{5,6},{6,5},{7,4},{8,11},{9,10},{10,... | collective-permute-start | bytes 248840 | tf_op jit(solution)/shard_map/ppermute | solution.py:105
  139.3 10.7 %collective-permute-start.17 = (f32[162,128]{1,0:T(8,128)S(1)}, f32[162,128]{1,0:T(8,128)S(1)}, u32[]{:S(2)}, u32[]{:S(2)}) collective-permute-start(f32[162,128]{1,0:T(8,128)S(1)} %add.462), channel_id=1, source_target_pairs={{0,3},{1,2},{2,1},{3,0},{4,7},{5,6},{6,5},{7,4},{8,11},{9,10},{10,... | collective-permute-start | bytes 248840 | tf_op jit(solution)/shard_map/ppermute | solution.py:105
  141.2 10.6 %collective-permute-start.9 = (f32[162,128]{1,0:T(8,128)S(1)}, f32[162,128]{1,0:T(8,128)S(1)}, u32[]{:S(2)}, u32[]{:S(2)}) collective-permute-start(f32[162,128]{1,0:T(8,128)S(1)} %add.446), channel_id=1, source_target_pairs={{0,3},{1,2},{2,1},{3,0},{4,7},{5,6},{6,5},{7,4},{8,11},{9,10},{10,... | collective-permute-start | bytes 248840 | tf_op jit(solution)/shard_map/ppermute | solution.py:105
  146.6 8.9 %collective-permute-start.26 = (f32[162,128]{1,0:T(8,128)S(1)}, f32[162,128]{1,0:T(8,128)S(1)}, u32[]{:S(2)}, u32[]{:S(2)}) collective-permute-start(f32[162,128]{1,0:T(8,128)S(1)} %add.479), channel_id=1, source_target_pairs={{0,7},{1,6},{2,5},{3,4},{4,3},{5,2},{6,1},{7,0},{8,15},{9,14},{10,... | collective-permute-start | bytes 248840 | tf_op jit(solution)/shard_map/ppermute | solution.py:105
  150.0 8.6 %collective-permute-start.18 = (f32[162,128]{1,0:T(8,128)S(1)}, f32[162,128]{1,0:T(8,128)S(1)}, u32[]{:S(2)}, u32[]{:S(2)}) collective-permute-start(f32[162,128]{1,0:T(8,128)S(1)} %add.463), channel_id=1, source_target_pairs={{0,7},{1,6},{2,5},{3,4},{4,3},{5,2},{6,1},{7,0},{8,15},{9,14},{10,... | collective-permute-start | bytes 248840 | tf_op jit(solution)/shard_map/ppermute | solution.py:105
  151.8 8.9 %collective-permute-start.10 = (f32[162,128]{1,0:T(8,128)S(1)}, f32[162,128]{1,0:T(8,128)S(1)}, u32[]{:S(2)}, u32[]{:S(2)}) collective-permute-start(f32[162,128]{1,0:T(8,128)S(1)} %add.447), channel_id=1, source_target_pairs={{0,7},{1,6},{2,5},{3,4},{4,3},{5,2},{6,1},{7,0},{8,15},{9,14},{10,... | collective-permute-start | bytes 248840 | tf_op jit(solution)/shard_map/ppermute | solution.py:105
  155.5 7.9 %collective-permute-start.27 = (f32[162,128]{1,0:T(8,128)S(1)}, f32[162,128]{1,0:T(8,128)S(1)}, u32[]{:S(2)}, u32[]{:S(2)}) collective-permute-start(f32[162,128]{1,0:T(8,128)S(1)} %add.480), channel_id=1, source_target_pairs={{0,8},{1,9},{2,10},{3,11},{4,12},{5,13},{6,14},{7,15},{8,0},{9,1},... | collective-permute-start | bytes 248840 | tf_op jit(solution)/shard_map/ppermute | solution.py:105
  158.6 6.1 %collective-permute-start.19 = (f32[162,128]{1,0:T(8,128)S(1)}, f32[162,128]{1,0:T(8,128)S(1)}, u32[]{:S(2)}, u32[]{:S(2)}) collective-permute-start(f32[162,128]{1,0:T(8,128)S(1)} %add.464), channel_id=1, source_target_pairs={{0,8},{1,9},{2,10},{3,11},{4,12},{5,13},{6,14},{7,15},{8,0},{9,1},... | collective-permute-start | bytes 248840 | tf_op jit(solution)/shard_map/ppermute | solution.py:105
  160.7 6.1 %collective-permute-start.11 = (f32[162,128]{1,0:T(8,128)S(1)}, f32[162,128]{1,0:T(8,128)S(1)}, u32[]{:S(2)}, u32[]{:S(2)}) collective-permute-start(f32[162,128]{1,0:T(8,128)S(1)} %add.448), channel_id=1, source_target_pairs={{0,8},{1,9},{2,10},{3,11},{4,12},{5,13},{6,14},{7,15},{8,0},{9,1},... | collective-permute-start | bytes 248840 | tf_op jit(solution)/shard_map/ppermute | solution.py:105
  (19 other events, 28.0 us)
